TPU v7x, 256 devices: a whole 4x4x8 slice. The times are simulated.
256 devices in a mesh: row: 16 (over x, y_hi, core), col: 16 (over y_lo, z).
Axes of the slice: x: 4, y: 4 (y_hi: 2, y_lo: 2; y = y_hi * 2 + y_lo), z: 8, core: 2. Of those that a mesh axis runs over, the one named last changes fastest.
Arguments:
- left_rows: float32 [1024, 61440], P('col', 'row'), may hold values from -1.2 to 1.2
- right_cols: float32 [61440, 4096], P('col', 'row'), may hold values from -1.2 to 1.2
- left_pattern: int32 [16, 240], replicated, may hold values from 0 to 1, as said below
- right_pattern: int32 [240, 16], replicated, may hold values from 0 to 1, as said below
Outputs:
- square_terms: float32 [1024, 4096], P('col', 'row')
Inputs may be any that keep to these rules, and one draw needn't show every extreme that they name: Every device's tile of left_pattern (row b, inner blocks from a * 15) has between 1 and 3 occupied blocks, and some tile has exactly 3 in every draw. Every device's tile of right_pattern (inner blocks from b * 15, column a) has between 1 and 3 occupied blocks, and some tile has exactly 3 in every draw.
All inputs are finite; a program needn't handle non-finite values.
Results may differ from a plain program's by a relative error of at most 0.0001.
Values sent between devices are 32-bit elements; how exact they have to be, the bound alone decides.
No kernel may reach another device: no remote copies, remote signals or barrier semaphores. Data moves between devices by JAX's collectives and lax.ppermute only.
A program may use at most 128 MiB of HBM per device.

v0:
```python
import jax
import jax.numpy as jnp
from jax import lax
from jax.sharding import PartitionSpec as P


STEPS = 4
CAP = 3
QUAD = 4


def slots(flags, cap):
    full = (flags != 0).astype(jnp.int32)
    width = full.shape[-1]
    where = jnp.arange(width, dtype=jnp.int32)
    before = (where[None, :] < where[:, None]).astype(jnp.int32)
    rank = jnp.sum(full[:, None, :] * before[None, :, :], axis=-1)
    hit = (full[:, None, :] == 1) & (rank[:, None, :] == jnp.arange(cap, dtype=jnp.int32)[None, :, None])
    index = jnp.sum(jnp.where(hit, where[None, None, :], 0), axis=-1)
    return index, jnp.any(hit, axis=-1)


def pick_cols(x, index, blk):
    return jnp.concatenate(
        [lax.dynamic_slice_in_dim(x, index[s] * blk, blk, axis=1) for s in range(index.shape[0])], axis=1
    )


def pick_rows(x, index, blk):
    return jnp.concatenate(
        [lax.dynamic_slice_in_dim(x, index[s] * blk, blk, axis=0) for s in range(index.shape[0])], axis=0
    )


def aligned_right(right, lidx, lok, ridx, rok, blk):
    weight = ((lidx[:, None] == ridx[None, :]) & lok[:, None] & rok[None, :]).astype(right.dtype)
    blocks = right.reshape(ridx.shape[0], blk, right.shape[1])
    picked = jnp.einsum("ij,jab->iab", weight, blocks, precision=lax.Precision.HIGHEST)
    return picked.reshape(right.shape)


def flat_pairs(moves, ncol):
    return [(sr * ncol + sc, dr * ncol + dc) for (sr, sc), (dr, dc) in moves]


def spread_roots(left_small, coldev, rowdev, nrow, ncol):
    flat = ("row", "col")
    received = []
    for hop in range(1, nrow // QUAD):
        moves = []
        for c in range(ncol):
            for k in range(STEPS):
                root = (c + k) % nrow
                moves.append(((root, c), ((root + QUAD * hop) % nrow, c)))
        received.append(lax.ppermute(left_small, flat, flat_pairs(moves, ncol)))
    held = received[0]
    for more in received[1:]:
        held = held + more
    is_root = ((rowdev - coldev) % nrow) < STEPS
    return jnp.where(is_root, left_small, held)


def gather_lefts(held, yhi, nrow, ncol):
    flat = ("row", "col")
    received = []
    for j in range(2):
        moves = []
        for q in range(ncol):
            for x in range(nrow // QUAD):
                for k in range(QUAD):
                    target = x * QUAD + ((k // 2 + j) % 2) * 2 + k % 2
                    moves.append(((x * QUAD + q % QUAD, (q - k) % ncol), (target, q)))
        received.append(lax.ppermute(held, flat, flat_pairs(moves, ncol)))
    near = jnp.where(yhi == 0, received[0], received[1])
    far = jnp.where(yhi == 0, received[1], received[0])
    return near, far


def send_home(part, near_k, to_partner, nrow, ncol):
    flat = ("row", "col")
    moves = []
    for r in range(nrow):
        for q in range(ncol):
            moves.append(((r, q), (r ^ 1 if to_partner else r, (q - r % 2 - near_k) % ncol)))
    return lax.ppermute(part, flat, flat_pairs(moves, ncol))


def steps(left_rows, right_cols, left_pattern, right_pattern):
    nrow = lax.axis_size("row")
    ncol = lax.axis_size("col")
    assert nrow == ncol and nrow % QUAD == 0 and STEPS == QUAD == 4
    _, left_width = left_rows.shape
    right_height, blk = right_cols.shape
    per_k = left_width // blk
    trows = right_height // blk
    rowdev = lax.axis_index("row")
    coldev = lax.axis_index("col")
    core = rowdev % 2
    yhi = (rowdev // 2) % 2

    tiles = left_pattern.reshape(ncol, nrow, per_k)
    grid_rows = jnp.stack([coldev] + [(coldev - k) % ncol for k in range(STEPS)])
    panels = jnp.stack([rowdev] + [coldev] * STEPS)
    rights = right_pattern.reshape(ncol, trows, nrow)
    flags = jnp.concatenate([tiles[grid_rows, panels], rights[coldev, :, rowdev][None]], axis=0)
    index, ok = slots(flags, CAP)
    own_left = index[0]
    lidx, lok = index[1:1 + STEPS], ok[1:1 + STEPS]
    ridx, rok = index[1 + STEPS], ok[1 + STEPS]

    left_small = pick_cols(left_rows, own_left, blk)
    right_small = pick_rows(right_cols, ridx, blk)
    highest = lax.Precision.HIGHEST

    def ordered_for(k):
        kl = lax.dynamic_index_in_dim(lidx, k, axis=0, keepdims=False)
        kok = lax.dynamic_index_in_dim(lok, k, axis=0, keepdims=False)
        return aligned_right(right_small, kl, kok, ridx, rok, blk)

    for_partner = jnp.stack([ordered_for(1 - core), ordered_for(3 - core)])
    from_partner = lax.ppermute(for_partner, "row", [(r, r ^ 1) for r in range(nrow)])
    plans = [
        (0, False, ordered_for(core)),
        (2, False, ordered_for(core + 2)),
        (0, True, from_partner[0]),
        (2, True, from_partner[1]),
    ]

    held = spread_roots(left_small, coldev, rowdev, nrow, ncol)
    near, far = gather_lefts(held, yhi, nrow, ncol)

    total = None
    for near_k, to_partner, right in plans:
        left = near if near_k == 0 else far
        part = jnp.dot(left, right, precision=highest, preferred_element_type=jnp.float32)
        part = send_home(part, near_k, to_partner, nrow, ncol)
        total = part if total is None else total + part
    return total


def solution(mesh):
    return jax.shard_map(
        steps,
        mesh=mesh,
        in_specs=(P("col", "row"), P("col", "row"), P(), P()),
        out_specs=P("col", "row"),
        check_vma=False,
    )
```

profile of v0, /device:TPU:9, one launch (start us, length us, event | category | flops | bytes accessed | tf_op | source)
XLA Modules:
  0.0 77.7 jit_solution(5551591718098197238)
XLA Ops:
  0.0 0.8 %reshape.499 = s32[16,16,15]{2,1,0:T(8,128)S(1)} reshape(s32[16,240]{1,0:T(8,128)} %param.6) | data formatting | bytes 30720 | tf_op jit(solution)/shard_map/reshape | solution.py:101
  0.8 0.8 %reshape.500 = s32[16,15,16]{1,0,2:T(8,128)S(1)} reshape(s32[240,16]{0,1:T(8,128)} %param.7) | data formatting | bytes 30720 | tf_op jit(solution)/shard_map/reshape | solution.py:104
  1.7 0.1 stack.38
  1.8 0.1 stack.36
  1.9 0.6 gather_fusion
  2.6 0.2 multiply_reduce_fusion
  2.7 0.2 fusion.13
  2.9 0.2 select_reduce_fusion
  3.0 0.7 fusion.64
  5.6 0.1 slice.52
  5.7 0.1 slice.54
  5.7 0.3 fusion.21
  6.0 0.3 fusion.17
  6.3 1.2 %constant_dynamic-slice_fusion.8 = (f32[256,256]{1,0:T(8,128)S(1)}, f32[256,256]{1,0:T(8,128)S(1)}, f32[256,256]{1,0:T(8,128)S(1)}) fusion(f32[3840,256]{1,0:T(8,128)} %param.5, s32[]{:T(128)S(6)} %select_n.140, s32[]{:T(128)S(6)} %select_n.142, s32[]{:T(128)S(6)} %select_n.141), kind=kLoop, calls=%fused_computation.39 | loop fusion | bytes 1572876 | tf_op jit(solution)/shard_map/dynamic_slice | solution.py:31
  7.5 0.1 pad_maximum_fusion.1
  7.5 1.5 %fusion.2 = f32[3,256,256]{2,0,1:T(4,128)S(1)} fusion(f32[3,256,256]{2,1,0:T(8,128)S(1)} %bitcast.43, s32[3]{0:T(128)S(1)} %get-tuple-element.27, pred[3]{0:T(512)(128)(4,1)S(1)} %get-tuple-element.11, s32[3]{0:T(128)S(1)} %get-tuple-element.7, pred[3]{0:T(512)(128)(4,1)S(1)} %get-tuple-element.28), kind=kOutput, calls=%fused_computation.4 | convolution fusion | flops 7077915 | bytes 1572894 | tf_op jit(solution)/shard_map/ij,jab->iab/dot_general | solution.py:38
  9.0 0.2 copy.27
  9.2 1.5 %fusion = f32[3,256,256]{2,0,1:T(4,128)S(1)} fusion(f32[3,256,256]{2,1,0:T(8,128)S(1)} %bitcast.44, s32[3]{0:T(128)S(1)} %get-tuple-element.27, pred[3]{0:T(512)(128)(4,1)S(1)} %get-tuple-element.10, s32[3]{0:T(128)S(1)} %get-tuple-element.6, pred[3]{0:T(512)(128)(4,1)S(1)} %get-tuple-element.28), kind=kOutput, calls=%fused_computation.2 | convolution fusion | flops 7077915 | bytes 1572894 | tf_op jit(solution)/shard_map/ij,jab->iab/dot_general | solution.py:38
  10.7 0.2 copy.29
  10.8 1.3 %pad_maximum_fusion = f32[2,768,256]{2,1,0:T(8,128)} fusion(f32[1,768,256]{2,1,0:T(8,128)S(1)} %bitcast.50, f32[1,768,256]{2,1,0:T(8,128)S(1)} %bitcast.49), kind=kLoop, calls=%fused_computation.1 | loop fusion | flops 393216 | bytes 3145728 | tf_op jit(solution)/shard_map/stack | solution.py:120
  12.1 0.7 collective-permute-start.7
  14.7 0.9 %constant_dynamic-slice_fusion.13 = (f32[64,256]{1,0:T(8,128)S(1)}, f32[64,256]{1,0:T(8,128)S(1)}, f32[64,256]{1,0:T(8,128)S(1)}) fusion(f32[64,3840]{1,0:T(8,128)} %param.4, s32[]{:T(128)S(6)} %select_n.133, s32[]{:T(128)S(6)} %select_n.135, s32[]{:T(128)S(6)} %select_n.134), kind=kLoop, calls=%fused_computation.44 | loop fusion | bytes 393228 | tf_op jit(solution)/shard_map/dynamic_slice | solution.py:25
  15.6 0.7 pad_maximum_fusion.2
  16.3 0.7 collective-permute-start
  17.0 1.3 %collective-permute-start.1 = (f32[64,768]{1,0:T(8,128)}, f32[64,768]{1,0:T(8,128)}, u32[]{:S(2)}, u32[]{:S(2)}) collective-permute-start(f32[64,768]{1,0:T(8,128)} %pad_maximum_fusion.2), channel_id=1, source_target_pairs={{0,128},{16,144},{32,160},{48,176},{17,145},{33,161},{49,177},{65,... | collective-permute-start | bytes 589832 | tf_op jit(solution)/shard_map/ppermute | solution.py:55
  18.3 1.3 %collective-permute-start.2 = (f32[64,768]{1,0:T(8,128)}, f32[64,768]{1,0:T(8,128)}, u32[]{:S(2)}, u32[]{:S(2)}) collective-permute-start(f32[64,768]{1,0:T(8,128)} %pad_maximum_fusion.2), channel_id=1, source_target_pairs={{0,192},{16,208},{32,224},{48,240},{17,209},{33,225},{49,241},{65,... | collective-permute-start | bytes 589832 | tf_op jit(solution)/shard_map/ppermute | solution.py:55
  19.6 1.5 %fusion.4 = f32[3,256,256]{2,0,1:T(4,128)S(1)} fusion(f32[3,256,256]{2,1,0:T(8,128)S(1)} %bitcast.45, s32[3]{0:T(128)S(1)} %get-tuple-element.27, pred[3]{0:T(512)(128)(4,1)S(1)} %get-tuple-element.9, s32[3]{0:T(128)S(1)} %get-tuple-element.5, pred[3]{0:T(512)(128)(4,1)S(1)} %get-tuple-element.28), kind=kOutput, calls=%fused_computation.6 | convolution fusion | flops 7077915 | bytes 1572894 | tf_op jit(solution)/shard_map/ij,jab->iab/dot_general | solution.py:38
  21.1 0.2 copy.25
  21.3 0.0 collective-permute-done
  21.3 10.0 %collective-permute-done.1 = f32[64,768]{1,0:T(8,128)} collective-permute-done((f32[64,768]{1,0:T(8,128)}, f32[64,768]{1,0:T(8,128)}, u32[]{:S(2)}, u32[]{:S(2)}) %collective-permute-start.1) | collective-permute-done | bytes 196640 | tf_op jit(solution)/shard_map/ppermute | solution.py:55
  31.3 0.0 collective-permute-done.2
  31.3 1.1 %add_select_fusion = f32[64,768]{1,0:T(8,128)S(1)} fusion(f32[64,768]{1,0:T(8,128)} %collective-permute-done.2, f32[64,768]{1,0:T(8,128)S(1)} %collective-permute-done, f32[64,768]{1,0:T(8,128)} %collective-permute-done.1, pred[]{:T(512)S(6)} %lt.110, f32[64,256]{1,0:T(8,128)S(1)} %get-tuple-element.19, f32[64,256]{1,0:T(8,128)S(1)} %get-tuple-element.20, ...), kind=kLoop, calls=%fused_computation.16 | loop fusion | flops 245760 | bytes 983041 | tf_op jit(solution)/shard_map/jit(_where)/select_n | solution.py:60
  32.4 1.9 %collective-permute-start.3 = (f32[64,768]{1,0:T(8,128)S(1)}, f32[64,768]{1,0:T(8,128)S(1)}, u32[]{:S(2)}, u32[]{:S(2)}) collective-permute-start(f32[64,768]{1,0:T(8,128)S(1)} %add_select_fusion), channel_id=1, source_target_pairs={{0,0},{15,16},{14,32},{13,48},{64,64},{79,80},{78,96},{77,112},{12... | collective-permute-start | bytes 589832 | tf_op jit(solution)/shard_map/ppermute | solution.py:73
  34.3 5.3 %collective-permute-start.4 = (f32[64,768]{1,0:T(8,128)S(1)}, f32[64,768]{1,0:T(8,128)S(1)}, u32[]{:S(2)}, u32[]{:S(2)}) collective-permute-start(f32[64,768]{1,0:T(8,128)S(1)} %add_select_fusion), channel_id=1, source_target_pairs={{0,32},{15,48},{14,0},{13,16},{64,96},{79,112},{78,64},{77,80},{12... | collective-permute-start | bytes 589832 | tf_op jit(solution)/shard_map/ppermute | solution.py:73
  39.7 1.5 %fusion.6 = f32[3,256,256]{2,0,1:T(4,128)S(1)} fusion(f32[3,256,256]{2,1,0:T(8,128)S(1)} %bitcast.46, s32[3]{0:T(128)S(1)} %get-tuple-element.27, pred[3]{0:T(512)(128)(4,1)S(1)} %get-tuple-element.28, pred[3]{0:T(512)(128)(4,1)S(1)} %get-tuple-element.12, s32[3]{0:T(128)S(1)} %get-tuple-element.8), kind=kOutput, calls=%fused_computation.8 | convolution fusion | flops 7077915 | bytes 1572894 | tf_op jit(solution)/shard_map/ij,jab->iab/dot_general | solution.py:38
  41.2 0.2 copy.23
  41.3 16.7 %collective-permute-done.3 = f32[64,768]{1,0:T(8,128)S(1)} collective-permute-done((f32[64,768]{1,0:T(8,128)S(1)}, f32[64,768]{1,0:T(8,128)S(1)}, u32[]{:S(2)}, u32[]{:S(2)}) %collective-permute-start.3) | collective-permute-done | bytes 196640 | tf_op jit(solution)/shard_map/ppermute | solution.py:73
  58.0 0.0 collective-permute-done.4
  58.0 0.5 fusion.11
  58.6 2.8 %collective-permute-start.6 = (f32[64,256]{1,0:T(8,128)S(1)}, f32[64,256]{1,0:T(8,128)S(1)}, u32[]{:S(2)}, u32[]{:S(2)}) collective-permute-start(f32[64,256]{1,0:T(8,128)S(1)} %fusion.11), channel_id=1, source_target_pairs={{0,14},{1,15},{2,0},{3,1},{4,2},{5,3},{6,4},{7,5},{8,6},{9,7},{10,... | collective-permute-start | bytes 196616 | tf_op jit(solution)/shard_map/ppermute | solution.py:85
  61.4 0.5 fusion.10
  61.9 3.5 %collective-permute-start.5 = (f32[64,256]{1,0:T(8,128)S(1)}, f32[64,256]{1,0:T(8,128)S(1)}, u32[]{:S(2)}, u32[]{:S(2)}) collective-permute-start(f32[64,256]{1,0:T(8,128)S(1)} %fusion.10), channel_id=1, source_target_pairs={{0,0},{1,1},{2,2},{3,3},{4,4},{5,5},{6,6},{7,7},{8,8},{9,9},{10,10... | collective-permute-start | bytes 196616 | tf_op jit(solution)/shard_map/ppermute | solution.py:85
  65.4 0.0 collective-permute-done.7
  65.5 0.5 fusion.9
  66.0 5.2 %collective-permute-start.8 = (f32[64,256]{1,0:T(8,128)S(1)}, f32[64,256]{1,0:T(8,128)S(1)}, u32[]{:S(2)}, u32[]{:S(2)}) collective-permute-start(f32[64,256]{1,0:T(8,128)S(1)} %fusion.9), channel_id=1, source_target_pairs={{0,16},{1,17},{2,18},{3,19},{4,20},{5,21},{6,22},{7,23},{8,24},{9,... | collective-permute-start | bytes 196616 | tf_op jit(solution)/shard_map/ppermute | solution.py:85
  71.2 0.5 fusion.8
  71.7 0.1 collective-permute-start.9
  71.8 0.0 collective-permute-done.6
  71.8 0.0 collective-permute-done.5
  71.8 0.7 collective-permute-done.8
  72.5 4.6 %collective-permute-done.9 = f32[64,256]{1,0:T(8,128)S(1)} collective-permute-done((f32[64,256]{1,0:T(8,128)S(1)}, f32[64,256]{1,0:T(8,128)S(1)}, u32[]{:S(2)}, u32[]{:S(2)}) %collective-permute-start.9) | collective-permute-done | bytes 65568 | tf_op jit(solution)/shard_map/ppermute | solution.py:85
  77.0 0.6 add_add_fusion
  (4 shorter events, 0.0 us)
Async XLA Ops:
  12.1 53.3 %collective-permute-start.7 = (f32[2,768,256]{2,1,0:T(8,128)}, f32[2,768,256]{2,1,0:T(8,128)S(1)}, u32[]{:S(2)}, u32[]{:S(2)}) collective-permute-start(f32[2,768,256]{2,1,0:T(8,128)} %pad_maximum_fusion), channel_id=1, source_target_pairs={{0,16},{16,0},{32,48},{48,32},{64,80},{80,64},{96,112},{112,96},{1... | collective-permute-start | bytes 4718600 | tf_op jit(solution)/shard_map/ppermute | solution.py:121
  16.3 5.0 %collective-permute-start = (f32[64,768]{1,0:T(8,128)}, f32[64,768]{1,0:T(8,128)S(1)}, u32[]{:S(2)}, u32[]{:S(2)}) collective-permute-start(f32[64,768]{1,0:T(8,128)} %pad_maximum_fusion.2), channel_id=1, source_target_pairs={{0,64},{16,80},{32,96},{48,112},{17,81},{33,97},{49,113},{65,129},... | collective-permute-start | bytes 589832 | tf_op jit(solution)/shard_map/ppermute | solution.py:55
  17.0 14.4 %collective-permute-start.1 = (f32[64,768]{1,0:T(8,128)}, f32[64,768]{1,0:T(8,128)}, u32[]{:S(2)}, u32[]{:S(2)}) collective-permute-start(f32[64,768]{1,0:T(8,128)} %pad_maximum_fusion.2), channel_id=1, source_target_pairs={{0,128},{16,144},{32,160},{48,176},{17,145},{33,161},{49,177},{65,... | collective-permute-start | bytes 589832 | tf_op jit(solution)/shard_map/ppermute | solution.py:55
  18.3 13.1 %collective-permute-start.2 = (f32[64,768]{1,0:T(8,128)}, f32[64,768]{1,0:T(8,128)}, u32[]{:S(2)}, u32[]{:S(2)}) collective-permute-start(f32[64,768]{1,0:T(8,128)} %pad_maximum_fusion.2), channel_id=1, source_target_pairs={{0,192},{16,208},{32,224},{48,240},{17,209},{33,225},{49,241},{65,... | collective-permute-start | bytes 589832 | tf_op jit(solution)/shard_map/ppermute | solution.py:55
  32.4 25.6 %collective-permute-start.3 = (f32[64,768]{1,0:T(8,128)S(1)}, f32[64,768]{1,0:T(8,128)S(1)}, u32[]{:S(2)}, u32[]{:S(2)}) collective-permute-start(f32[64,768]{1,0:T(8,128)S(1)} %add_select_fusion), channel_id=1, source_target_pairs={{0,0},{15,16},{14,32},{13,48},{64,64},{79,80},{78,96},{77,112},{12... | collective-permute-start | bytes 589832 | tf_op jit(solution)/shard_map/ppermute | solution.py:73
  34.3 23.7 %collective-permute-start.4 = (f32[64,768]{1,0:T(8,128)S(1)}, f32[64,768]{1,0:T(8,128)S(1)}, u32[]{:S(2)}, u32[]{:S(2)}) collective-permute-start(f32[64,768]{1,0:T(8,128)S(1)} %add_select_fusion), channel_id=1, source_target_pairs={{0,32},{15,48},{14,0},{13,16},{64,96},{79,112},{78,64},{77,80},{12... | collective-permute-start | bytes 589832 | tf_op jit(solution)/shard_map/ppermute | solution.py:73
  58.6 13.2 %collective-permute-start.6 = (f32[64,256]{1,0:T(8,128)S(1)}, f32[64,256]{1,0:T(8,128)S(1)}, u32[]{:S(2)}, u32[]{:S(2)}) collective-permute-start(f32[64,256]{1,0:T(8,128)S(1)} %fusion.11), channel_id=1, source_target_pairs={{0,14},{1,15},{2,0},{3,1},{4,2},{5,3},{6,4},{7,5},{8,6},{9,7},{10,... | collective-permute-start | bytes 196616 | tf_op jit(solution)/shard_map/ppermute | solution.py:85
  61.9 9.9 %collective-permute-start.5 = (f32[64,256]{1,0:T(8,128)S(1)}, f32[64,256]{1,0:T(8,128)S(1)}, u32[]{:S(2)}, u32[]{:S(2)}) collective-permute-start(f32[64,256]{1,0:T(8,128)S(1)} %fusion.10), channel_id=1, source_target_pairs={{0,0},{1,1},{2,2},{3,3},{4,4},{5,5},{6,6},{7,7},{8,8},{9,9},{10,10... | collective-permute-start | bytes 196616 | tf_op jit(solution)/shard_map/ppermute | solution.py:85
  66.0 6.5 %collective-permute-start.8 = (f32[64,256]{1,0:T(8,128)S(1)}, f32[64,256]{1,0:T(8,128)S(1)}, u32[]{:S(2)}, u32[]{:S(2)}) collective-permute-start(f32[64,256]{1,0:T(8,128)S(1)} %fusion.9), channel_id=1, source_target_pairs={{0,16},{1,17},{2,18},{3,19},{4,20},{5,21},{6,22},{7,23},{8,24},{9,... | collective-permute-start | bytes 196616 | tf_op jit(solution)/shard_map/ppermute | solution.py:85
  71.7 5.4 %collective-permute-start.9 = (f32[64,256]{1,0:T(8,128)S(1)}, f32[64,256]{1,0:T(8,128)S(1)}, u32[]{:S(2)}, u32[]{:S(2)}) collective-permute-start(f32[64,256]{1,0:T(8,128)S(1)} %fusion.8), channel_id=1, source_target_pairs={{0,30},{1,31},{2,16},{3,17},{4,18},{5,19},{6,20},{7,21},{8,22},{9,... | collective-permute-start | bytes 196616 | tf_op jit(solution)/shard_map/ppermute | solution.py:85
where the time goes:
time: 78.1 us; the launch traced here: 77.7 us
  waiting for transfers between devices  32 us (41%)
  starting transfers between devices  22.8 us (29%)
  matrix products  8.05 us (10%)
  local copies, waits for them, and re-layouts  6.52 us (8%)
  other arithmetic  4.21 us (5%)
  between operations  4.06 us (5%)
    ppermute x2, waiting for transfers between devices, gather_lefts(): received.append(lax.ppermute(held, flat, flat_pairs(moves, ncol)))  16.7 us
    ppermute x4, starting transfers between devices, send_home(): return lax.ppermute(part, flat, flat_pairs(moves, ncol))  11.6 us
    ppermute x3, waiting for transfers between devices, spread_roots(): received.append(lax.ppermute(left_small, flat, flat_pairs(moves, ncol)))  10 us
    ppermute x2, starting transfers between devices, gather_lefts(): received.append(lax.ppermute(held, flat, flat_pairs(moves, ncol)))  7.23 us
    dot_general x4, matrix products, aligned_right(): jnp.einsum('ij,jab->iab', weight, blocks, precision=lax.Precision.HIGHEST)  5.99 us
    ppermute x4, waiting for transfers between devices, send_home(): return lax.ppermute(part, flat, flat_pairs(moves, ncol))  5.27 us
    ppermute x3, starting transfers between devices, spread_roots(): received.append(lax.ppermute(left_small, flat, flat_pairs(moves, ncol)))  3.29 us
    dot_general x4, matrix products, steps(): jnp.dot(left, right, precision=highest, preferred_element_type=jnp.float32)  2.06 us
  transfers between devices with their start and end apart: 10, of which 4 were waited for; matrix products, arithmetic and copies ran while one was open for 10% of the time, Pallas kernels for 0%

commit v1 on v0

--- a/solution.py
+++ b/solution.py
@@ -98,11 +98,11 @@
     core = rowdev % 2
     yhi = (rowdev // 2) % 2
 
-    tiles = left_pattern.reshape(ncol, nrow, per_k)
     grid_rows = jnp.stack([coldev] + [(coldev - k) % ncol for k in range(STEPS)])
     panels = jnp.stack([rowdev] + [coldev] * STEPS)
-    rights = right_pattern.reshape(ncol, trows, nrow)
-    flags = jnp.concatenate([tiles[grid_rows, panels], rights[coldev, :, rowdev][None]], axis=0)
+    lefts = left_pattern[grid_rows[:, None], panels[:, None] * per_k + jnp.arange(per_k)[None, :]]
+    own_right = lax.dynamic_slice(right_pattern, (coldev * trows, rowdev), (trows, 1)).reshape(1, trows)
+    flags = jnp.concatenate([lefts, own_right], axis=0)
     index, ok = slots(flags, CAP)
     own_left = index[0]
     lidx, lok = index[1:1 + STEPS], ok[1:1 + STEPS]
@@ -119,12 +119,8 @@
 
     for_partner = jnp.stack([ordered_for(1 - core), ordered_for(3 - core)])
     from_partner = lax.ppermute(for_partner, "row", [(r, r ^ 1) for r in range(nrow)])
-    plans = [
-        (0, False, ordered_for(core)),
-        (2, False, ordered_for(core + 2)),
-        (0, True, from_partner[0]),
-        (2, True, from_partner[1]),
-    ]
+    own_near, own_far = ordered_for(core), ordered_for(core + 2)
+    plans = [(0, False, own_near), (2, False, own_far), (0, True, from_partner[0]), (2, True, from_partner[1])]
 
     held = spread_roots(left_small, coldev, rowdev, nrow, ncol)
     near, far = gather_lefts(held, yhi, nrow, ncol)

time: 78.1 us -> 80.2 us (1.027)
  local copies, waits for them, and re-layouts: 6.52 us -> 8.57 us
    reshape x2 -> x0, local copies, waits for them, and re-layouts: 1.63 us -> none  [the longest x1 0.82 us: steps(): rights = right_pattern.reshape(ncol, trows, nrow)]
    gather x1 -> x2, local copies, waits for them, and re-layouts: 0.6 us -> 2.15 us  [steps(): left_pattern[grid_rows[:, None], panels[:, None] * per_k + jnp.arange(per...]
    concatenate x1 -> x2, local copies, waits for them, and re-layouts: 0.01 us -> 0.85 us  [the longest x1 0.77 us: steps(): flags = jnp.concatenate([lefts, own_right], axis=0)]
  transfers between devices with their start and end apart: 10 -> 10, of which waited for: 4 -> 4; matrix products, arithmetic and copies ran while one was open for 10% -> 11% of each run, Pallas kernels for 0% -> 0%
where the time goes in v1:
time: 80.2 us; the launch traced here: 79.8 us
  waiting for transfers between devices  31.4 us (39%)
  starting transfers between devices  22.8 us (28%)
  matrix products  8.74 us (11%)
  local copies, waits for them, and re-layouts  8.57 us (11%)
  other arithmetic  4.28 us (5%)
  between operations  4.02 us (5%)
    ppermute x2, waiting for transfers between devices, gather_lefts(): received.append(lax.ppermute(held, flat, flat_pairs(moves, ncol)))  16 us
    ppermute x4, starting transfers between devices, send_home(): return lax.ppermute(part, flat, flat_pairs(moves, ncol))  11.6 us
    ppermute x3, waiting for transfers between devices, spread_roots(): received.append(lax.ppermute(left_small, flat, flat_pairs(moves, ncol)))  10.1 us
    ppermute x2, starting transfers between devices, gather_lefts(): received.append(lax.ppermute(held, flat, flat_pairs(moves, ncol)))  7.19 us
    dot_general x4, matrix products, aligned_right(): jnp.einsum('ij,jab->iab', weight, blocks, precision=lax.Precision.HIGHEST)  6.68 us
    ppermute x4, waiting for transfers between devices, send_home(): return lax.ppermute(part, flat, flat_pairs(moves, ncol))  5.29 us
    ppermute x3, starting transfers between devices, spread_roots(): received.append(lax.ppermute(left_small, flat, flat_pairs(moves, ncol)))  3.29 us
    gather x2, local copies, waits for them, and re-layouts, steps(): left_pattern[grid_rows[:, None], panels[:, None] * per_k + jnp.arange(per...  2.15 us
  transfers between devices with their start and end apart: 10, of which 4 were waited for; matrix products, arithmetic and copies ran while one was open for 11% of the time, Pallas kernels for 0%

profile of v1, /device:TPU:9, one launch (start us, length us, event | category | flops | bytes accessed | tf_op | source)
XLA Modules:
  0.0 79.8 jit_solution(10087703467701910196)
XLA Ops:
  0.0 0.0 copy-start
  0.0 0.1 stack.36
  0.1 0.1 stack.38
  0.2 0.1 fusion.17
  0.3 0.1 reshape.289
  0.4 0.3 copy-done
  0.7 2.1 %gather_fusion = s32[75]{0:T(128)S(1)} fusion(s32[16,240]{1,0:T(8,128)S(1)} %copy-done, s32[75]{0:T(128)S(1)} %reshape.289), kind=kCustom, calls=%fused_computation | custom fusion | bytes 1200 | tf_op jit(solution)/shard_map/gather | solution.py:103
  2.8 0.1 reshape.292
  2.9 0.8 dynamic-slice_bitcast_fusion
  3.7 0.2 multiply_reduce_fusion
  3.8 0.2 select_reduce_fusion
  4.0 0.7 fusion.62
  6.6 0.1 fusion.13
  6.7 0.1 slice.52
  6.8 0.1 slice.54
  6.9 0.7 fusion.24
  7.6 0.0 copy-start.1
  7.6 0.7 fusion.20
  8.3 0.0 copy-start.2
  8.3 1.2 %constant_dynamic-slice_fusion.8 = (f32[256,256]{1,0:T(8,128)S(1)}, f32[256,256]{1,0:T(8,128)S(1)}, f32[256,256]{1,0:T(8,128)S(1)}) fusion(f32[3840,256]{1,0:T(8,128)} %param.5, s32[]{:T(128)S(6)} %select_n.138, s32[]{:T(128)S(6)} %select_n.140, s32[]{:T(128)S(6)} %select_n.139), kind=kLoop, calls=%fused_computation.43 | loop fusion | bytes 1572876 | tf_op jit(solution)/shard_map/dynamic_slice | solution.py:31
  9.5 0.1 pad_maximum_fusion.1
  9.6 1.5 %fusion.2 = f32[3,256,256]{2,0,1:T(4,128)S(1)} fusion(f32[3,256,256]{2,1,0:T(8,128)S(1)} %bitcast.41, s32[3]{0:T(128)S(1)} %get-tuple-element.27, pred[3]{0:T(512)(128)(4,1)S(1)} %get-tuple-element.11, s32[3]{0:T(128)S(1)} %get-tuple-element.7, pred[3]{0:T(512)(128)(4,1)S(1)} %get-tuple-element.28), kind=kOutput, calls=%fused_computation.4 | convolution fusion | flops 7077915 | bytes 1572894 | tf_op jit(solution)/shard_map/ij,jab->iab/dot_general | solution.py:38
  11.1 0.2 copy.26
  11.3 1.5 %fusion = f32[3,256,256]{2,0,1:T(4,128)S(1)} fusion(f32[3,256,256]{2,1,0:T(8,128)S(1)} %bitcast.42, s32[3]{0:T(128)S(1)} %get-tuple-element.27, pred[3]{0:T(512)(128)(4,1)S(1)} %get-tuple-element.10, s32[3]{0:T(128)S(1)} %get-tuple-element.6, pred[3]{0:T(512)(128)(4,1)S(1)} %get-tuple-element.28), kind=kOutput, calls=%fused_computation.2 | convolution fusion | flops 7077915 | bytes 1572894 | tf_op jit(solution)/shard_map/ij,jab->iab/dot_general | solution.py:38
  12.8 0.2 copy.28
  12.9 1.3 %pad_maximum_fusion = f32[2,768,256]{2,1,0:T(8,128)} fusion(f32[1,768,256]{2,1,0:T(8,128)S(1)} %bitcast.48, f32[1,768,256]{2,1,0:T(8,128)S(1)} %bitcast.47), kind=kLoop, calls=%fused_computation.1 | loop fusion | flops 393216 | bytes 3145728 | tf_op jit(solution)/shard_map/stack | solution.py:120
  14.2 0.7 collective-permute-start.7
  16.7 0.9 %constant_dynamic-slice_fusion.13 = (f32[64,256]{1,0:T(8,128)S(1)}, f32[64,256]{1,0:T(8,128)S(1)}, f32[64,256]{1,0:T(8,128)S(1)}) fusion(f32[64,3840]{1,0:T(8,128)} %param.4, s32[]{:T(128)S(6)} %select_n.131, s32[]{:T(128)S(6)} %select_n.133, s32[]{:T(128)S(6)} %select_n.132), kind=kLoop, calls=%fused_computation.48 | loop fusion | bytes 393228 | tf_op jit(solution)/shard_map/dynamic_slice | solution.py:25
  17.7 0.7 pad_maximum_fusion.2
  18.4 0.7 collective-permute-start
  19.0 1.3 %collective-permute-start.1 = (f32[64,768]{1,0:T(8,128)}, f32[64,768]{1,0:T(8,128)}, u32[]{:S(2)}, u32[]{:S(2)}) collective-permute-start(f32[64,768]{1,0:T(8,128)} %pad_maximum_fusion.2), channel_id=1, source_target_pairs={{0,128},{16,144},{32,160},{48,176},{17,145},{33,161},{49,177},{65,... | collective-permute-start | bytes 589832 | tf_op jit(solution)/shard_map/ppermute | solution.py:55
  20.3 1.3 %collective-permute-start.2 = (f32[64,768]{1,0:T(8,128)}, f32[64,768]{1,0:T(8,128)}, u32[]{:S(2)}, u32[]{:S(2)}) collective-permute-start(f32[64,768]{1,0:T(8,128)} %pad_maximum_fusion.2), channel_id=1, source_target_pairs={{0,192},{16,208},{32,224},{48,240},{17,209},{33,225},{49,241},{65,... | collective-permute-start | bytes 589832 | tf_op jit(solution)/shard_map/ppermute | solution.py:55
  21.7 0.0 copy-done.1
  21.7 0.0 copy-done.2
  21.7 1.5 %fusion.4 = f32[3,256,256]{2,0,1:T(4,128)S(1)} fusion(f32[3,256,256]{2,1,0:T(8,128)S(1)} %bitcast.43, s32[3]{0:T(128)S(1)} %get-tuple-element.27, pred[3]{0:T(512)(128)(4,1)S(1)} %get-tuple-element.9, s32[3]{0:T(128)S(1)} %get-tuple-element.5, pred[3]{0:T(512)(128)(4,1)S(1)} %get-tuple-element.28), kind=kOutput, calls=%fused_computation.6 | convolution fusion | flops 7077915 | bytes 1572894 | tf_op jit(solution)/shard_map/ij,jab->iab/dot_general | solution.py:38
  23.2 0.2 copy.24
  23.3 0.0 collective-permute-done
  23.4 10.1 %collective-permute-done.1 = f32[64,768]{1,0:T(8,128)} collective-permute-done((f32[64,768]{1,0:T(8,128)}, f32[64,768]{1,0:T(8,128)}, u32[]{:S(2)}, u32[]{:S(2)}) %collective-permute-start.1) | collective-permute-done | bytes 196640 | tf_op jit(solution)/shard_map/ppermute | solution.py:55
  33.4 0.0 collective-permute-done.2
  33.4 1.1 %add_select_fusion = f32[64,768]{1,0:T(8,128)S(1)} fusion(f32[64,768]{1,0:T(8,128)} %collective-permute-done.2, f32[64,768]{1,0:T(8,128)S(1)} %collective-permute-done, f32[64,768]{1,0:T(8,128)} %collective-permute-done.1, pred[]{:T(512)S(6)} %lt.113, f32[64,256]{1,0:T(8,128)S(1)} %get-tuple-element.19, f32[64,256]{1,0:T(8,128)S(1)} %get-tuple-element.20, ...), kind=kLoop, calls=%fused_computation.16 | loop fusion | flops 245760 | bytes 983041 | tf_op jit(solution)/shard_map/jit(_where)/select_n | solution.py:60
  34.5 1.9 %collective-permute-start.3 = (f32[64,768]{1,0:T(8,128)S(1)}, f32[64,768]{1,0:T(8,128)S(1)}, u32[]{:S(2)}, u32[]{:S(2)}) collective-permute-start(f32[64,768]{1,0:T(8,128)S(1)} %add_select_fusion), channel_id=1, source_target_pairs={{0,0},{15,16},{14,32},{13,48},{64,64},{79,80},{78,96},{77,112},{12... | collective-permute-start | bytes 589832 | tf_op jit(solution)/shard_map/ppermute | solution.py:73
  36.4 5.3 %collective-permute-start.4 = (f32[64,768]{1,0:T(8,128)S(1)}, f32[64,768]{1,0:T(8,128)S(1)}, u32[]{:S(2)}, u32[]{:S(2)}) collective-permute-start(f32[64,768]{1,0:T(8,128)S(1)} %add_select_fusion), channel_id=1, source_target_pairs={{0,32},{15,48},{14,0},{13,16},{64,96},{79,112},{78,64},{77,80},{12... | collective-permute-start | bytes 589832 | tf_op jit(solution)/shard_map/ppermute | solution.py:73
  41.7 2.2 %fusion.6 = f32[3,256,256]{2,0,1:T(4,128)S(1)} fusion(f32[3,256,256]{2,1,0:T(8,128)S(1)} %bitcast.44, s32[3]{0:T(128)} %copy-done.2, pred[3]{0:T(512)(128)(4,1)} %copy-done.1, pred[3]{0:T(512)(128)(4,1)} %get-tuple-element.12, s32[3]{0:T(128)} %get-tuple-element.8), kind=kOutput, calls=%fused_computation.8 | convolution fusion | flops 7077915 | bytes 1572894 | tf_op jit(solution)/shard_map/ij,jab->iab/dot_general | solution.py:38
  43.9 0.2 copy.22
  44.1 16.0 %collective-permute-done.3 = f32[64,768]{1,0:T(8,128)S(1)} collective-permute-done((f32[64,768]{1,0:T(8,128)S(1)}, f32[64,768]{1,0:T(8,128)S(1)}, u32[]{:S(2)}, u32[]{:S(2)}) %collective-permute-start.3) | collective-permute-done | bytes 196640 | tf_op jit(solution)/shard_map/ppermute | solution.py:73
  60.1 0.0 collective-permute-done.4
  60.1 0.5 fusion.11
  60.6 2.9 %collective-permute-start.6 = (f32[64,256]{1,0:T(8,128)S(1)}, f32[64,256]{1,0:T(8,128)S(1)}, u32[]{:S(2)}, u32[]{:S(2)}) collective-permute-start(f32[64,256]{1,0:T(8,128)S(1)} %fusion.11), channel_id=1, source_target_pairs={{0,14},{1,15},{2,0},{3,1},{4,2},{5,3},{6,4},{7,5},{8,6},{9,7},{10,... | collective-permute-start | bytes 196616 | tf_op jit(solution)/shard_map/ppermute | solution.py:85
  63.5 0.5 fusion.10
  64.0 3.5 %collective-permute-start.5 = (f32[64,256]{1,0:T(8,128)S(1)}, f32[64,256]{1,0:T(8,128)S(1)}, u32[]{:S(2)}, u32[]{:S(2)}) collective-permute-start(f32[64,256]{1,0:T(8,128)S(1)} %fusion.10), channel_id=1, source_target_pairs={{0,0},{1,1},{2,2},{3,3},{4,4},{5,5},{6,6},{7,7},{8,8},{9,9},{10,10... | collective-permute-start | bytes 196616 | tf_op jit(solution)/shard_map/ppermute | solution.py:85
  67.5 0.0 collective-permute-done.7
  67.5 0.5 fusion.9
  68.0 5.2 %collective-permute-start.8 = (f32[64,256]{1,0:T(8,128)S(1)}, f32[64,256]{1,0:T(8,128)S(1)}, u32[]{:S(2)}, u32[]{:S(2)}) collective-permute-start(f32[64,256]{1,0:T(8,128)S(1)} %fusion.9), channel_id=1, source_target_pairs={{0,16},{1,17},{2,18},{3,19},{4,20},{5,21},{6,22},{7,23},{8,24},{9,... | collective-permute-start | bytes 196616 | tf_op jit(solution)/shard_map/ppermute | solution.py:85
  73.2 0.5 fusion.8
  73.7 0.1 collective-permute-start.9
  73.8 0.0 collective-permute-done.6
  73.8 0.0 collective-permute-done.5
  73.8 0.7 collective-permute-done.8
  74.6 4.6 %collective-permute-done.9 = f32[64,256]{1,0:T(8,128)S(1)} collective-permute-done((f32[64,256]{1,0:T(8,128)S(1)}, f32[64,256]{1,0:T(8,128)S(1)}, u32[]{:S(2)}, u32[]{:S(2)}) %collective-permute-start.9) | collective-permute-done | bytes 65568 | tf_op jit(solution)/shard_map/ppermute | solution.py:85
  79.1 0.6 add_add_fusion
  (4 shorter events, 0.0 us)
Async XLA Ops:
  0.0 0.7 copy-start
  7.6 14.1 %copy-start.1 = (pred[3]{0:T(512)(128)(4,1)}, pred[3]{0:T(512)(128)(4,1)S(1)}, u32[]{:S(2)}) copy-start(pred[3]{0:T(512)(128)(4,1)S(1)} %get-tuple-element.28) | copy-start | bytes 13
  8.3 13.3 %copy-start.2 = (s32[3]{0:T(128)}, s32[3]{0:T(128)S(1)}, u32[]{:S(2)}) copy-start(s32[3]{0:T(128)S(1)} %get-tuple-element.27) | copy-start | bytes 40
  14.2 53.3 %collective-permute-start.7 = (f32[2,768,256]{2,1,0:T(8,128)}, f32[2,768,256]{2,1,0:T(8,128)S(1)}, u32[]{:S(2)}, u32[]{:S(2)}) collective-permute-start(f32[2,768,256]{2,1,0:T(8,128)} %pad_maximum_fusion), channel_id=1, source_target_pairs={{0,16},{16,0},{32,48},{48,32},{64,80},{80,64},{96,112},{112,96},{1... | collective-permute-start | bytes 4718600 | tf_op jit(solution)/shard_map/ppermute | solution.py:121
  18.4 5.0 %collective-permute-start = (f32[64,768]{1,0:T(8,128)}, f32[64,768]{1,0:T(8,128)S(1)}, u32[]{:S(2)}, u32[]{:S(2)}) collective-permute-start(f32[64,768]{1,0:T(8,128)} %pad_maximum_fusion.2), channel_id=1, source_target_pairs={{0,64},{16,80},{32,96},{48,112},{17,81},{33,97},{49,113},{65,129},... | collective-permute-start | bytes 589832 | tf_op jit(solution)/shard_map/ppermute | solution.py:55
  19.0 14.4 %collective-permute-start.1 = (f32[64,768]{1,0:T(8,128)}, f32[64,768]{1,0:T(8,128)}, u32[]{:S(2)}, u32[]{:S(2)}) collective-permute-start(f32[64,768]{1,0:T(8,128)} %pad_maximum_fusion.2), channel_id=1, source_target_pairs={{0,128},{16,144},{32,160},{48,176},{17,145},{33,161},{49,177},{65,... | collective-permute-start | bytes 589832 | tf_op jit(solution)/shard_map/ppermute | solution.py:55
  20.3 13.1 %collective-permute-start.2 = (f32[64,768]{1,0:T(8,128)}, f32[64,768]{1,0:T(8,128)}, u32[]{:S(2)}, u32[]{:S(2)}) collective-permute-start(f32[64,768]{1,0:T(8,128)} %pad_maximum_fusion.2), channel_id=1, source_target_pairs={{0,192},{16,208},{32,224},{48,240},{17,209},{33,225},{49,241},{65,... | collective-permute-start | bytes 589832 | tf_op jit(solution)/shard_map/ppermute | solution.py:55
  34.5 25.6 %collective-permute-start.3 = (f32[64,768]{1,0:T(8,128)S(1)}, f32[64,768]{1,0:T(8,128)S(1)}, u32[]{:S(2)}, u32[]{:S(2)}) collective-permute-start(f32[64,768]{1,0:T(8,128)S(1)} %add_select_fusion), channel_id=1, source_target_pairs={{0,0},{15,16},{14,32},{13,48},{64,64},{79,80},{78,96},{77,112},{12... | collective-permute-start | bytes 589832 | tf_op jit(solution)/shard_map/ppermute | solution.py:73
  36.4 23.7 %collective-permute-start.4 = (f32[64,768]{1,0:T(8,128)S(1)}, f32[64,768]{1,0:T(8,128)S(1)}, u32[]{:S(2)}, u32[]{:S(2)}) collective-permute-start(f32[64,768]{1,0:T(8,128)S(1)} %add_select_fusion), channel_id=1, source_target_pairs={{0,32},{15,48},{14,0},{13,16},{64,96},{79,112},{78,64},{77,80},{12... | collective-permute-start | bytes 589832 | tf_op jit(solution)/shard_map/ppermute | solution.py:73
  60.6 13.2 %collective-permute-start.6 = (f32[64,256]{1,0:T(8,128)S(1)}, f32[64,256]{1,0:T(8,128)S(1)}, u32[]{:S(2)}, u32[]{:S(2)}) collective-permute-start(f32[64,256]{1,0:T(8,128)S(1)} %fusion.11), channel_id=1, source_target_pairs={{0,14},{1,15},{2,0},{3,1},{4,2},{5,3},{6,4},{7,5},{8,6},{9,7},{10,... | collective-permute-start | bytes 196616 | tf_op jit(solution)/shard_map/ppermute | solution.py:85
  64.0 9.8 %collective-permute-start.5 = (f32[64,256]{1,0:T(8,128)S(1)}, f32[64,256]{1,0:T(8,128)S(1)}, u32[]{:S(2)}, u32[]{:S(2)}) collective-permute-start(f32[64,256]{1,0:T(8,128)S(1)} %fusion.10), channel_id=1, source_target_pairs={{0,0},{1,1},{2,2},{3,3},{4,4},{5,5},{6,6},{7,7},{8,8},{9,9},{10,10... | collective-permute-start | bytes 196616 | tf_op jit(solution)/shard_map/ppermute | solution.py:85
  68.0 6.5 %collective-permute-start.8 = (f32[64,256]{1,0:T(8,128)S(1)}, f32[64,256]{1,0:T(8,128)S(1)}, u32[]{:S(2)}, u32[]{:S(2)}) collective-permute-start(f32[64,256]{1,0:T(8,128)S(1)} %fusion.9), channel_id=1, source_target_pairs={{0,16},{1,17},{2,18},{3,19},{4,20},{5,21},{6,22},{7,23},{8,24},{9,... | collective-permute-start | bytes 196616 | tf_op jit(solution)/shard_map/ppermute | solution.py:85
  73.7 5.4 %collective-permute-start.9 = (f32[64,256]{1,0:T(8,128)S(1)}, f32[64,256]{1,0:T(8,128)S(1)}, u32[]{:S(2)}, u32[]{:S(2)}) collective-permute-start(f32[64,256]{1,0:T(8,128)S(1)} %fusion.8), channel_id=1, source_target_pairs={{0,30},{1,31},{2,16},{3,17},{4,18},{5,19},{6,20},{7,21},{8,22},{9,... | collective-permute-start | bytes 196616 | tf_op jit(solution)/shard_map/ppermute | solution.py:85

commit v2 on v1

--- a/solution.py
+++ b/solution.py
@@ -60,7 +60,7 @@
     return jnp.where(is_root, left_small, held)
 
 
-def gather_lefts(held, yhi, nrow, ncol):
+def gather_lefts(held, nrow, ncol):
     flat = ("row", "col")
     received = []
     for j in range(2):
@@ -71,17 +71,19 @@
                     target = x * QUAD + ((k // 2 + j) % 2) * 2 + k % 2
                     moves.append(((x * QUAD + q % QUAD, (q - k) % ncol), (target, q)))
         received.append(lax.ppermute(held, flat, flat_pairs(moves, ncol)))
-    near = jnp.where(yhi == 0, received[0], received[1])
-    far = jnp.where(yhi == 0, received[1], received[0])
-    return near, far
+    return received
 
 
-def send_home(part, near_k, to_partner, nrow, ncol):
+def tile_of(row, j):
+    return row % 2 + 2 * (((row // 2) % 2 + j) % 2)
+
+
+def send_home(part, j, to_partner, nrow, ncol):
     flat = ("row", "col")
     moves = []
     for r in range(nrow):
         for q in range(ncol):
-            moves.append(((r, q), (r ^ 1 if to_partner else r, (q - r % 2 - near_k) % ncol)))
+            moves.append(((r, q), (r ^ 1 if to_partner else r, (q - tile_of(r, j)) % ncol)))
     return lax.ppermute(part, flat, flat_pairs(moves, ncol))
 
 
@@ -95,18 +97,15 @@
     trows = right_height // blk
     rowdev = lax.axis_index("row")
     coldev = lax.axis_index("col")
-    core = rowdev % 2
-    yhi = (rowdev // 2) % 2
 
-    grid_rows = jnp.stack([coldev] + [(coldev - k) % ncol for k in range(STEPS)])
-    panels = jnp.stack([rowdev] + [coldev] * STEPS)
-    lefts = left_pattern[grid_rows[:, None], panels[:, None] * per_k + jnp.arange(per_k)[None, :]]
+    own_flags = lax.dynamic_slice(left_pattern, (coldev, rowdev * per_k), (1, per_k))
+    own_left = slots(own_flags, CAP)[0][0]
+    grid_rows = jnp.stack([(coldev - k) % ncol for k in range(STEPS)])
+    lefts = left_pattern[grid_rows[:, None], coldev * per_k + jnp.arange(per_k)[None, :]]
     own_right = lax.dynamic_slice(right_pattern, (coldev * trows, rowdev), (trows, 1)).reshape(1, trows)
-    flags = jnp.concatenate([lefts, own_right], axis=0)
-    index, ok = slots(flags, CAP)
-    own_left = index[0]
-    lidx, lok = index[1:1 + STEPS], ok[1:1 + STEPS]
-    ridx, rok = index[1 + STEPS], ok[1 + STEPS]
+    index, ok = slots(jnp.concatenate([lefts, own_right], axis=0), CAP)
+    lidx, lok = index[:STEPS], ok[:STEPS]
+    ridx, rok = index[STEPS], ok[STEPS]
 
     left_small = pick_cols(left_rows, own_left, blk)
     right_small = pick_rows(right_cols, ridx, blk)
@@ -117,20 +116,19 @@
         kok = lax.dynamic_index_in_dim(lok, k, axis=0, keepdims=False)
         return aligned_right(right_small, kl, kok, ridx, rok, blk)
 
-    for_partner = jnp.stack([ordered_for(1 - core), ordered_for(3 - core)])
+    for_partner = jnp.stack([ordered_for(tile_of(rowdev ^ 1, j)) for j in range(2)])
     from_partner = lax.ppermute(for_partner, "row", [(r, r ^ 1) for r in range(nrow)])
-    own_near, own_far = ordered_for(core), ordered_for(core + 2)
-    plans = [(0, False, own_near), (2, False, own_far), (0, True, from_partner[0]), (2, True, from_partner[1])]
+    own = [ordered_for(tile_of(rowdev, j)) for j in range(2)]
 
     held = spread_roots(left_small, coldev, rowdev, nrow, ncol)
-    near, far = gather_lefts(held, yhi, nrow, ncol)
+    received = gather_lefts(held, nrow, ncol)
 
     total = None
-    for near_k, to_partner, right in plans:
-        left = near if near_k == 0 else far
-        part = jnp.dot(left, right, precision=highest, preferred_element_type=jnp.float32)
-        part = send_home(part, near_k, to_partner, nrow, ncol)
-        total = part if total is None else total + part
+    for j in range(2):
+        for to_partner, right in ((False, own[j]), (True, from_partner[j])):
+            part = jnp.dot(received[j], right, precision=highest, preferred_element_type=jnp.float32)
+            part = send_home(part, j, to_partner, nrow, ncol)
+            total = part if total is None else total + part
     return total
 
 

time: 80.2 us -> 80.5 us (level)
  local copies, waits for them, and re-layouts: 8.57 us -> 5.72 us
  starting transfers between devices: 22.8 us -> 24.9 us
  matrix products: 8.74 us -> 10.3 us
    dot_general x4, matrix products: 2.06 us -> 4.29 us  [steps(): jnp.dot(received[j], right, precision=highest, preferred_element_type=jnp...]
    dynamic_slice x2 -> x0, local copies, waits for them, and re-layouts: 1.48 us -> none  [the longest x1 0.74 us: ordered_for(): kl = lax.dynamic_index_in_dim(lidx, k, axis=0, keepdims=False)]
    ppermute x4, starting transfers between devices: 11.6 us -> 13 us  [send_home(): return lax.ppermute(part, flat, flat_pairs(moves, ncol))]
    another operation x1, other arithmetic: 1.26 us -> 0.1 us  [steps(): jnp.stack([ordered_for(tile_of(rowdev ^ 1, j)) for j in range(2)])]
    gather x2, local copies, waits for them, and re-layouts: 2.15 us -> 1.13 us  [steps(): left_pattern[grid_rows[:, None], coldev * per_k + jnp.arange(per_k)[None,...]
  transfers between devices with their start and end apart: 10 -> 10, of which waited for: 4 -> 3; matrix products, arithmetic and copies ran while one was open for 11% -> 15% of each run, Pallas kernels for 0% -> 0%
where the time goes in v2:
time: 80.5 us; the launch traced here: 79.9 us
  waiting for transfers between devices  31 us (39%)
  starting transfers between devices  24.9 us (31%)
  matrix products  10.3 us (13%)
  local copies, waits for them, and re-layouts  5.72 us (7%)
  between operations  4.03 us (5%)
  other arithmetic  4 us (5%)
    ppermute x2, waiting for transfers between devices, gather_lefts(): received.append(lax.ppermute(held, flat, flat_pairs(moves, ncol)))  16.7 us
    ppermute x4, starting transfers between devices, send_home(): return lax.ppermute(part, flat, flat_pairs(moves, ncol))  13 us
    ppermute x3, waiting for transfers between devices, spread_roots(): received.append(lax.ppermute(left_small, flat, flat_pairs(moves, ncol)))  9.36 us
    ppermute x2, starting transfers between devices, gather_lefts(): received.append(lax.ppermute(held, flat, flat_pairs(moves, ncol)))  7.2 us
    dot_general x4, matrix products, aligned_right(): jnp.einsum('ij,jab->iab', weight, blocks, precision=lax.Precision.HIGHEST)  5.99 us
    ppermute x4, waiting for transfers between devices, send_home(): return lax.ppermute(part, flat, flat_pairs(moves, ncol))  4.94 us
    dot_general x4, matrix products, steps(): jnp.dot(received[j], right, precision=highest, preferred_element_type=jnp...  4.29 us
    ppermute x3, starting transfers between devices, spread_roots(): received.append(lax.ppermute(left_small, flat, flat_pairs(moves, ncol)))  3.98 us
  transfers between devices with their start and end apart: 10, of which 3 were waited for; matrix products, arithmetic and copies ran while one was open for 15% of the time, Pallas kernels for 0%

profile of v2, /device:TPU:9, one launch (start us, length us, event | category | flops | bytes accessed | tf_op | source)
XLA Modules:
  0.0 79.9 jit_solution(7254283904970871145)
XLA Ops:
  0.0 0.0 copy-start
  0.0 0.0 copy-start.1
  0.1 0.1 fusion.54
  0.1 0.1 broadcast_or_fusion
  0.2 0.1 reshape.328
  0.3 0.4 copy-done.1
  0.7 1.0 %gather_fusion = s32[60]{0:T(128)S(1)} fusion(s32[16,240]{1,0:T(8,128)S(1)} %copy-done.1, s32[60]{0:T(128)S(1)} %reshape.328), kind=kCustom, calls=%fused_computation | custom fusion | bytes 960 | tf_op jit(solution)/shard_map/gather | solution.py:104
  1.8 0.1 reshape.331
  1.9 0.0 copy-done
  1.9 0.1 dynamic-slice_bitcast_fusion
  2.0 0.2 multiply_reduce_fusion
  2.1 0.2 fusion.13
  2.3 0.2 select_reduce_fusion
  2.5 0.6 fusion.62
  5.0 1.2 %constant_dynamic-slice_fusion.8 = (f32[256,256]{1,0:T(8,128)S(1)}, f32[256,256]{1,0:T(8,128)S(1)}, f32[256,256]{1,0:T(8,128)S(1)}) fusion(f32[3840,256]{1,0:T(8,128)} %param.5, s32[]{:T(128)S(6)} %select_n.182, s32[]{:T(128)S(6)} %select_n.184, s32[]{:T(128)S(6)} %select_n.183), kind=kLoop, calls=%fused_computation.38 | loop fusion | bytes 1572876 | tf_op jit(solution)/shard_map/dynamic_slice | solution.py:31
  6.2 0.1 pad_maximum_fusion.1
  6.2 1.5 %fusion.4 = f32[3,256,256]{2,0,1:T(4,128)S(1)} fusion(f32[3,256,256]{2,1,0:T(8,128)S(1)} %bitcast.67, s32[3]{0:T(128)S(1)} %get-tuple-element.30, pred[3]{0:T(512)(128)(4,1)S(1)} %get-tuple-element.25, s32[3]{0:T(128)S(1)} %get-tuple-element.21, pred[3]{0:T(512)(128)(4,1)S(1)} %get-tuple-element.29), kind=kOutput, calls=%fused_computation.6 | convolution fusion | flops 7077915 | bytes 1572894 | tf_op jit(solution)/shard_map/ij,jab->iab/dot_general | solution.py:38
  7.7 0.2 copy.16
  7.9 1.5 %fusion.2 = f32[3,256,256]{2,0,1:T(4,128)S(1)} fusion(f32[3,256,256]{2,1,0:T(8,128)S(1)} %bitcast.68, s32[3]{0:T(128)S(1)} %get-tuple-element.30, pred[3]{0:T(512)(128)(4,1)S(1)} %get-tuple-element.24, s32[3]{0:T(128)S(1)} %get-tuple-element.20, pred[3]{0:T(512)(128)(4,1)S(1)} %get-tuple-element.29), kind=kOutput, calls=%fused_computation.4 | convolution fusion | flops 7077915 | bytes 1572894 | tf_op jit(solution)/shard_map/ij,jab->iab/dot_general | solution.py:38
  9.4 0.2 copy.18
  9.6 0.1 pad_maximum_fusion
  9.7 0.7 collective-permute-start.5
  10.4 0.1 broadcast_compare_fusion.1
  10.5 0.4 fusion.12
  10.9 0.2 fusion.35
  11.0 0.6 fusion.63
  13.6 0.9 %constant_dynamic-slice_fusion.13 = (f32[64,256]{1,0:T(8,128)S(1)}, f32[64,256]{1,0:T(8,128)S(1)}, f32[64,256]{1,0:T(8,128)S(1)}) fusion(f32[64,3840]{1,0:T(8,128)} %param.4, s32[]{:T(128)S(6)} %select_n.164, s32[]{:T(128)S(6)} %select_n.166, s32[]{:T(128)S(6)} %select_n.165), kind=kLoop, calls=%fused_computation.43 | loop fusion | bytes 393228 | tf_op jit(solution)/shard_map/dynamic_slice | solution.py:25
  14.5 0.7 pad_maximum_fusion.2
  15.2 1.3 %collective-permute-start = (f32[64,768]{1,0:T(8,128)}, f32[64,768]{1,0:T(8,128)}, u32[]{:S(2)}, u32[]{:S(2)}) collective-permute-start(f32[64,768]{1,0:T(8,128)} %pad_maximum_fusion.2), channel_id=1, source_target_pairs={{0,64},{16,80},{32,96},{48,112},{17,81},{33,97},{49,113},{65,129},... | collective-permute-start | bytes 589832 | tf_op jit(solution)/shard_map/ppermute | solution.py:55
  16.6 1.3 %collective-permute-start.1 = (f32[64,768]{1,0:T(8,128)}, f32[64,768]{1,0:T(8,128)}, u32[]{:S(2)}, u32[]{:S(2)}) collective-permute-start(f32[64,768]{1,0:T(8,128)} %pad_maximum_fusion.2), channel_id=1, source_target_pairs={{0,128},{16,144},{32,160},{48,176},{17,145},{33,161},{49,177},{65,... | collective-permute-start | bytes 589832 | tf_op jit(solution)/shard_map/ppermute | solution.py:55
  17.9 1.4 %collective-permute-start.2 = (f32[64,768]{1,0:T(8,128)}, f32[64,768]{1,0:T(8,128)}, u32[]{:S(2)}, u32[]{:S(2)}) collective-permute-start(f32[64,768]{1,0:T(8,128)} %pad_maximum_fusion.2), channel_id=1, source_target_pairs={{0,192},{16,208},{32,224},{48,240},{17,209},{33,225},{49,241},{65,... | collective-permute-start | bytes 589832 | tf_op jit(solution)/shard_map/ppermute | solution.py:55
  19.2 1.5 %fusion.6 = f32[3,256,256]{2,0,1:T(4,128)S(1)} fusion(f32[3,256,256]{2,1,0:T(8,128)S(1)} %bitcast.69, s32[3]{0:T(128)S(1)} %get-tuple-element.30, pred[3]{0:T(512)(128)(4,1)S(1)} %get-tuple-element.29, pred[3]{0:T(512)(128)(4,1)S(1)} %get-tuple-element.22, s32[3]{0:T(128)S(1)} %get-tuple-element.18), kind=kOutput, calls=%fused_computation.8 | convolution fusion | flops 7077915 | bytes 1572894 | tf_op jit(solution)/shard_map/ij,jab->iab/dot_general | solution.py:38
  20.7 0.2 copy.14
  20.9 0.0 collective-permute-done
  20.9 9.4 %collective-permute-done.1 = f32[64,768]{1,0:T(8,128)} collective-permute-done((f32[64,768]{1,0:T(8,128)}, f32[64,768]{1,0:T(8,128)}, u32[]{:S(2)}, u32[]{:S(2)}) %collective-permute-start.1) | collective-permute-done | bytes 196640 | tf_op jit(solution)/shard_map/ppermute | solution.py:55
  30.3 0.0 collective-permute-done.2
  30.3 1.2 %add_select_fusion = f32[64,768]{1,0:T(8,128)S(1)} fusion(f32[64,768]{1,0:T(8,128)} %collective-permute-done.2, f32[64,768]{1,0:T(8,128)} %collective-permute-done, f32[64,768]{1,0:T(8,128)} %collective-permute-done.1, pred[]{:T(512)S(6)} %lt.165, f32[64,256]{1,0:T(8,128)S(1)} %get-tuple-element.11, f32[64,256]{1,0:T(8,128)S(1)} %get-tuple-element.12, ...), kind=kLoop, calls=%fused_computation.16 | loop fusion | flops 245760 | bytes 983041 | tf_op jit(solution)/shard_map/jit(_where)/select_n | solution.py:60
  31.4 1.9 %collective-permute-start.3 = (f32[64,768]{1,0:T(8,128)S(1)}, f32[64,768]{1,0:T(8,128)S(1)}, u32[]{:S(2)}, u32[]{:S(2)}) collective-permute-start(f32[64,768]{1,0:T(8,128)S(1)} %add_select_fusion), channel_id=1, source_target_pairs={{0,0},{15,16},{14,32},{13,48},{64,64},{79,80},{78,96},{77,112},{12... | collective-permute-start | bytes 589832 | tf_op jit(solution)/shard_map/ppermute | solution.py:73
  33.4 1.5 %fusion = f32[3,256,256]{2,0,1:T(4,128)S(1)} fusion(f32[3,256,256]{2,1,0:T(8,128)S(1)} %bitcast.70, s32[3]{0:T(128)S(1)} %get-tuple-element.30, pred[3]{0:T(512)(128)(4,1)S(1)} %get-tuple-element.23, s32[3]{0:T(128)S(1)} %get-tuple-element.19, pred[3]{0:T(512)(128)(4,1)S(1)} %get-tuple-element.29), kind=kOutput, calls=%fused_computation.2 | convolution fusion | flops 7077915 | bytes 1572894 | tf_op jit(solution)/shard_map/ij,jab->iab/dot_general | solution.py:38
  34.9 0.2 copy.20
  35.0 5.3 %collective-permute-start.7 = (f32[64,768]{1,0:T(8,128)S(1)}, f32[64,768]{1,0:T(8,128)S(1)}, u32[]{:S(2)}, u32[]{:S(2)}) collective-permute-start(f32[64,768]{1,0:T(8,128)S(1)} %add_select_fusion), channel_id=1, source_target_pairs={{0,32},{15,48},{14,0},{13,16},{64,96},{79,112},{78,64},{77,80},{12... | collective-permute-start | bytes 589832 | tf_op jit(solution)/shard_map/ppermute | solution.py:73
  40.3 16.7 %collective-permute-done.3 = f32[64,768]{1,0:T(8,128)S(1)} collective-permute-done((f32[64,768]{1,0:T(8,128)S(1)}, f32[64,768]{1,0:T(8,128)S(1)}, u32[]{:S(2)}, u32[]{:S(2)}) %collective-permute-start.3) | collective-permute-done | bytes 196640 | tf_op jit(solution)/shard_map/ppermute | solution.py:73
  57.0 0.5 fusion.64
  57.5 2.7 %collective-permute-start.4 = (f32[64,256]{1,0:T(8,128)S(1)}, f32[64,256]{1,0:T(8,128)S(1)}, u32[]{:S(2)}, u32[]{:S(2)}) collective-permute-start(f32[64,256]{1,0:T(8,128)S(1)} %fusion.64), channel_id=1, source_target_pairs={{0,0},{1,1},{2,2},{3,3},{4,4},{5,5},{6,6},{7,7},{8,8},{9,9},{10,10... | collective-permute-start | bytes 196616 | tf_op jit(solution)/shard_map/ppermute | solution.py:87
  60.2 0.0 collective-permute-done.7
  60.2 0.5 fusion.65
  60.7 2.2 %collective-permute-start.8 = (f32[64,256]{1,0:T(8,128)S(1)}, f32[64,256]{1,0:T(8,128)S(1)}, u32[]{:S(2)}, u32[]{:S(2)}) collective-permute-start(f32[64,256]{1,0:T(8,128)S(1)} %fusion.65), channel_id=1, source_target_pairs={{0,14},{1,15},{2,0},{3,1},{4,2},{5,3},{6,4},{7,5},{8,6},{9,7},{10,... | collective-permute-start | bytes 196616 | tf_op jit(solution)/shard_map/ppermute | solution.py:87
  62.9 0.0 collective-permute-done.5
  62.9 1.6 %fusion.9 = f32[64,256]{1,0:T(8,128)S(1)} fusion(f32[64,768]{1,0:T(8,128)S(1)} %collective-permute-done.3, f32[2,768,256]{2,1,0:T(8,128)} %collective-permute-done.5), kind=kOutput, calls=%fused_computation.13 | convolution fusion | flops 150994944 | bytes 1048576 | tf_op jit(solution)/shard_map/dot_general | solution.py:129
  64.5 8.1 %collective-permute-start.6 = (f32[64,256]{1,0:T(8,128)S(1)}, f32[64,256]{1,0:T(8,128)S(1)}, u32[]{:S(2)}, u32[]{:S(2)}) collective-permute-start(f32[64,256]{1,0:T(8,128)S(1)} %fusion.9), channel_id=1, source_target_pairs={{0,16},{1,17},{2,18},{3,19},{4,20},{5,21},{6,22},{7,23},{8,24},{9,... | collective-permute-start | bytes 196616 | tf_op jit(solution)/shard_map/ppermute | solution.py:87
  72.6 1.6 %fusion.8 = f32[64,256]{1,0:T(8,128)S(1)} fusion(f32[64,768]{1,0:T(8,128)S(1)} %collective-permute-done.7, f32[2,768,256]{2,1,0:T(8,128)} %collective-permute-done.5), kind=kOutput, calls=%fused_computation.11 | convolution fusion | flops 150994944 | bytes 1048576 | tf_op jit(solution)/shard_map/dot_general | solution.py:129
  74.2 0.1 collective-permute-start.9
  74.3 0.0 collective-permute-done.4
  74.3 0.0 collective-permute-done.8
  74.4 0.0 collective-permute-done.6
  74.4 4.9 %collective-permute-done.9 = f32[64,256]{1,0:T(8,128)S(1)} collective-permute-done((f32[64,256]{1,0:T(8,128)S(1)}, f32[64,256]{1,0:T(8,128)S(1)}, u32[]{:S(2)}, u32[]{:S(2)}) %collective-permute-start.9) | collective-permute-done | bytes 65568 | tf_op jit(solution)/shard_map/ppermute | solution.py:87
  79.3 0.6 add_add_fusion
  (7 shorter events, 0.1 us)
Async XLA Ops:
  0.0 1.9 %copy-start = (s32[240,16]{0,1:T(8,128)S(1)}, s32[240,16]{0,1:T(8,128)}, u32[]{:S(2)}) copy-start(s32[240,16]{0,1:T(8,128)} %param.7) | copy-start | bytes 46084
  0.0 0.7 copy-start.1
  9.7 53.2 %collective-permute-start.5 = (f32[2,768,256]{2,1,0:T(8,128)S(1)}, f32[2,768,256]{2,1,0:T(8,128)}, u32[]{:S(2)}, u32[]{:S(2)}) collective-permute-start(f32[2,768,256]{2,1,0:T(8,128)S(1)} %pad_maximum_fusion), channel_id=1, source_target_pairs={{0,16},{16,0},{32,48},{48,32},{64,80},{80,64},{96,112},{112,96},{1... | collective-permute-start | bytes 4718600 | tf_op jit(solution)/shard_map/ppermute | solution.py:120
  15.2 5.7 %collective-permute-start = (f32[64,768]{1,0:T(8,128)}, f32[64,768]{1,0:T(8,128)}, u32[]{:S(2)}, u32[]{:S(2)}) collective-permute-start(f32[64,768]{1,0:T(8,128)} %pad_maximum_fusion.2), channel_id=1, source_target_pairs={{0,64},{16,80},{32,96},{48,112},{17,81},{33,97},{49,113},{65,129},... | collective-permute-start | bytes 589832 | tf_op jit(solution)/shard_map/ppermute | solution.py:55
  16.6 13.7 %collective-permute-start.1 = (f32[64,768]{1,0:T(8,128)}, f32[64,768]{1,0:T(8,128)}, u32[]{:S(2)}, u32[]{:S(2)}) collective-permute-start(f32[64,768]{1,0:T(8,128)} %pad_maximum_fusion.2), channel_id=1, source_target_pairs={{0,128},{16,144},{32,160},{48,176},{17,145},{33,161},{49,177},{65,... | collective-permute-start | bytes 589832 | tf_op jit(solution)/shard_map/ppermute | solution.py:55
  17.9 12.4 %collective-permute-start.2 = (f32[64,768]{1,0:T(8,128)}, f32[64,768]{1,0:T(8,128)}, u32[]{:S(2)}, u32[]{:S(2)}) collective-permute-start(f32[64,768]{1,0:T(8,128)} %pad_maximum_fusion.2), channel_id=1, source_target_pairs={{0,192},{16,208},{32,224},{48,240},{17,209},{33,225},{49,241},{65,... | collective-permute-start | bytes 589832 | tf_op jit(solution)/shard_map/ppermute | solution.py:55
  31.4 25.6 %collective-permute-start.3 = (f32[64,768]{1,0:T(8,128)S(1)}, f32[64,768]{1,0:T(8,128)S(1)}, u32[]{:S(2)}, u32[]{:S(2)}) collective-permute-start(f32[64,768]{1,0:T(8,128)S(1)} %add_select_fusion), channel_id=1, source_target_pairs={{0,0},{15,16},{14,32},{13,48},{64,64},{79,80},{78,96},{77,112},{12... | collective-permute-start | bytes 589832 | tf_op jit(solution)/shard_map/ppermute | solution.py:73
  35.0 25.2 %collective-permute-start.7 = (f32[64,768]{1,0:T(8,128)S(1)}, f32[64,768]{1,0:T(8,128)S(1)}, u32[]{:S(2)}, u32[]{:S(2)}) collective-permute-start(f32[64,768]{1,0:T(8,128)S(1)} %add_select_fusion), channel_id=1, source_target_pairs={{0,32},{15,48},{14,0},{13,16},{64,96},{79,112},{78,64},{77,80},{12... | collective-permute-start | bytes 589832 | tf_op jit(solution)/shard_map/ppermute | solution.py:73
  57.5 16.8 %collective-permute-start.4 = (f32[64,256]{1,0:T(8,128)S(1)}, f32[64,256]{1,0:T(8,128)S(1)}, u32[]{:S(2)}, u32[]{:S(2)}) collective-permute-start(f32[64,256]{1,0:T(8,128)S(1)} %fusion.64), channel_id=1, source_target_pairs={{0,0},{1,1},{2,2},{3,3},{4,4},{5,5},{6,6},{7,7},{8,8},{9,9},{10,10... | collective-permute-start | bytes 196616 | tf_op jit(solution)/shard_map/ppermute | solution.py:87
  60.7 13.6 %collective-permute-start.8 = (f32[64,256]{1,0:T(8,128)S(1)}, f32[64,256]{1,0:T(8,128)S(1)}, u32[]{:S(2)}, u32[]{:S(2)}) collective-permute-start(f32[64,256]{1,0:T(8,128)S(1)} %fusion.65), channel_id=1, source_target_pairs={{0,14},{1,15},{2,0},{3,1},{4,2},{5,3},{6,4},{7,5},{8,6},{9,7},{10,... | collective-permute-start | bytes 196616 | tf_op jit(solution)/shard_map/ppermute | solution.py:87
  64.5 9.8 %collective-permute-start.6 = (f32[64,256]{1,0:T(8,128)S(1)}, f32[64,256]{1,0:T(8,128)S(1)}, u32[]{:S(2)}, u32[]{:S(2)}) collective-permute-start(f32[64,256]{1,0:T(8,128)S(1)} %fusion.9), channel_id=1, source_target_pairs={{0,16},{1,17},{2,18},{3,19},{4,20},{5,21},{6,22},{7,23},{8,24},{9,... | collective-permute-start | bytes 196616 | tf_op jit(solution)/shard_map/ppermute | solution.py:87
  74.2 5.1 %collective-permute-start.9 = (f32[64,256]{1,0:T(8,128)S(1)}, f32[64,256]{1,0:T(8,128)S(1)}, u32[]{:S(2)}, u32[]{:S(2)}) collective-permute-start(f32[64,256]{1,0:T(8,128)S(1)} %fusion.8), channel_id=1, source_target_pairs={{0,30},{1,31},{2,16},{3,17},{4,18},{5,19},{6,20},{7,21},{8,22},{9,... | collective-permute-start | bytes 196616 | tf_op jit(solution)/shard_map/ppermute | solution.py:87

commit v3 on v2

--- a/solution.py
+++ b/solution.py
@@ -7,6 +7,12 @@
 STEPS = 4
 CAP = 3
 QUAD = 4
+
+
+def shifted(value, axis, steps):
+    count = lax.axis_size(axis)
+    pairs = [(source, (source - steps) % count) for source in range(count)]
+    return lax.ppermute(value, axis, pairs)
 
 
 def slots(flags, cap):
@@ -60,7 +66,7 @@
     return jnp.where(is_root, left_small, held)
 
 
-def gather_lefts(held, nrow, ncol):
+def gather_lefts(held, yhi, nrow, ncol):
     flat = ("row", "col")
     received = []
     for j in range(2):
@@ -71,20 +77,9 @@
                     target = x * QUAD + ((k // 2 + j) % 2) * 2 + k % 2
                     moves.append(((x * QUAD + q % QUAD, (q - k) % ncol), (target, q)))
         received.append(lax.ppermute(held, flat, flat_pairs(moves, ncol)))
-    return received
-
-
-def tile_of(row, j):
-    return row % 2 + 2 * (((row // 2) % 2 + j) % 2)
-
-
-def send_home(part, j, to_partner, nrow, ncol):
-    flat = ("row", "col")
-    moves = []
-    for r in range(nrow):
-        for q in range(ncol):
-            moves.append(((r, q), (r ^ 1 if to_partner else r, (q - tile_of(r, j)) % ncol)))
-    return lax.ppermute(part, flat, flat_pairs(moves, ncol))
+    near = jnp.where(yhi == 0, received[0], received[1])
+    far = jnp.where(yhi == 0, received[1], received[0])
+    return near, far
 
 
 def steps(left_rows, right_cols, left_pattern, right_pattern):
@@ -97,6 +92,8 @@
     trows = right_height // blk
     rowdev = lax.axis_index("row")
     coldev = lax.axis_index("col")
+    core = rowdev % 2
+    yhi = (rowdev // 2) % 2
 
     own_flags = lax.dynamic_slice(left_pattern, (coldev, rowdev * per_k), (1, per_k))
     own_left = slots(own_flags, CAP)[0][0]
@@ -116,19 +113,24 @@
         kok = lax.dynamic_index_in_dim(lok, k, axis=0, keepdims=False)
         return aligned_right(right_small, kl, kok, ridx, rok, blk)
 
-    for_partner = jnp.stack([ordered_for(tile_of(rowdev ^ 1, j)) for j in range(2)])
-    from_partner = lax.ppermute(for_partner, "row", [(r, r ^ 1) for r in range(nrow)])
-    own = [ordered_for(tile_of(rowdev, j)) for j in range(2)]
+    ordered = [ordered_for(k) for k in range(STEPS)]
 
     held = spread_roots(left_small, coldev, rowdev, nrow, ncol)
-    received = gather_lefts(held, nrow, ncol)
+    near, far = gather_lefts(held, yhi, nrow, ncol)
+    swapped = lax.ppermute(jnp.stack([near, far]), "row", [(r, r ^ 1) for r in range(nrow)])
 
+    mine = core == 0
+    tiles = [
+        jnp.where(mine, near, swapped[0]),
+        jnp.where(mine, swapped[0], near),
+        jnp.where(mine, far, swapped[1]),
+        jnp.where(mine, swapped[1], far),
+    ]
     total = None
-    for j in range(2):
-        for to_partner, right in ((False, own[j]), (True, from_partner[j])):
-            part = jnp.dot(received[j], right, precision=highest, preferred_element_type=jnp.float32)
-            part = send_home(part, j, to_partner, nrow, ncol)
-            total = part if total is None else total + part
+    for k in range(STEPS):
+        part = jnp.dot(tiles[k], ordered[k], precision=highest, preferred_element_type=jnp.float32)
+        part = part if k == 0 else shifted(part, "col", k)
+        total = part if total is None else total + part
     return total
 
 

time: 80.5 us -> 70.8 us (0.88)
  the two profiles are of different devices: /device:TPU:9 before, /device:TPU:1 now
where the time goes in v3:
time: 70.8 us; the launch traced here: 70.2 us
  starting transfers between devices  24.6 us (35%)
  waiting for transfers between devices  19.5 us (28%)
  matrix products  12.4 us (18%)
  local copies, waits for them, and re-layouts  6.81 us (10%)
  between operations  3.91 us (6%)
  other arithmetic  2.97 us (4%)
    ppermute x2, waiting for transfers between devices, gather_lefts(): received.append(lax.ppermute(held, flat, flat_pairs(moves, ncol)))  17.2 us
    ppermute x3, starting transfers between devices, shifted(): return lax.ppermute(value, axis, pairs)  8.68 us
    ppermute x2, starting transfers between devices, gather_lefts(): received.append(lax.ppermute(held, flat, flat_pairs(moves, ncol)))  8.1 us
    ppermute x3, starting transfers between devices, spread_roots(): received.append(lax.ppermute(left_small, flat, flat_pairs(moves, ncol)))  7.81 us
    dot_general x4, matrix products, steps(): jnp.dot(tiles[k], ordered[k], precision=highest, preferred_element_type=j...  6.39 us
    dot_general x4, matrix products, aligned_right(): jnp.einsum('ij,jab->iab', weight, blocks, precision=lax.Precision.HIGHEST)  5.99 us
    ppermute x3, waiting for transfers between devices, shifted(): return lax.ppermute(value, axis, pairs)  2.32 us
    gather x2, local copies, waits for them, and re-layouts, steps(): left_pattern[grid_rows[:, None], coldev * per_k + jnp.arange(per_k)[None,...  1.84 us
  transfers between devices with their start and end apart: 9, of which 3 were waited for; matrix products, arithmetic and copies ran while one was open for 21% of the time, Pallas kernels for 0%

profile of v3, /device:TPU:1, one launch (start us, length us, event | category | flops | bytes accessed | tf_op | source)
XLA Modules:
  0.0 70.2 jit_solution(11422776344531287596)
XLA Ops:
  0.0 0.0 copy-start
  0.0 0.8 %broadcast_compare_fusion.1 = (pred[15]{0:T(512)(128)(4,1)S(1)}, s32[15]{0:T(128)S(1)}) fusion(s32[16,240]{1,0:T(8,128)} %param.6, s32[]{:T(128)S(6)} %select_n.149, s32[]{:T(128)S(6)} %select_n.150), kind=kLoop, calls=%fused_computation.103 | loop fusion | flops 45 | bytes 143 | tf_op jit(solution)/shard_map/eq | solution.py:24
  0.8 0.4 fusion.23
  1.2 0.2 fusion.42
  1.3 0.6 fusion.66
  3.7 0.9 %constant_dynamic-slice_fusion.5 = (f32[64,256]{1,0:T(8,128)S(1)}, f32[64,256]{1,0:T(8,128)S(1)}, f32[64,256]{1,0:T(8,128)S(1)}) fusion(f32[64,3840]{1,0:T(8,128)} %param.4, s32[]{:T(128)S(6)} %select_n.152, s32[]{:T(128)S(6)} %select_n.154, s32[]{:T(128)S(6)} %select_n.153), kind=kLoop, calls=%fused_computation.74 | loop fusion | bytes 393228 | tf_op jit(solution)/shard_map/dynamic_slice | solution.py:31
  4.7 5.2 %collective-permute-start.2 = (f32[64,768]{1,0:T(8,128)S(1)}, f32[64,768]{1,0:T(8,128)S(1)}, u32[]{:S(2)}, u32[]{:S(2)}) collective-permute-start(f32[64,768]{1,0:T(8,128)S(1)} %pad_maximum_fusion.2), channel_id=1, source_target_pairs={{0,192},{16,208},{32,224},{48,240},{17,209},{33,225},{49,241},{65,... | collective-permute-start | bytes 589832 | tf_op jit(solution)/shard_map/ppermute | solution.py:61
  9.9 1.3 %collective-permute-start = (f32[64,768]{1,0:T(8,128)S(1)}, f32[64,768]{1,0:T(8,128)S(1)}, u32[]{:S(2)}, u32[]{:S(2)}) collective-permute-start(f32[64,768]{1,0:T(8,128)S(1)} %pad_maximum_fusion.2), channel_id=1, source_target_pairs={{0,64},{16,80},{32,96},{48,112},{17,81},{33,97},{49,113},{65,129},... | collective-permute-start | bytes 589832 | tf_op jit(solution)/shard_map/ppermute | solution.py:61
  11.2 1.3 %collective-permute-start.1 = (f32[64,768]{1,0:T(8,128)S(1)}, f32[64,768]{1,0:T(8,128)S(1)}, u32[]{:S(2)}, u32[]{:S(2)}) collective-permute-start(f32[64,768]{1,0:T(8,128)S(1)} %pad_maximum_fusion.2), channel_id=1, source_target_pairs={{0,128},{16,144},{32,160},{48,176},{17,145},{33,161},{49,177},{65,... | collective-permute-start | bytes 589832 | tf_op jit(solution)/shard_map/ppermute | solution.py:61
  12.6 0.1 fusion.61
  12.7 0.1 broadcast_or_fusion
  12.7 0.1 reshape.336
  12.8 1.8 %gather_fusion = s32[60]{0:T(128)S(1)} fusion(s32[16,240]{1,0:T(8,128)} %param.6, s32[60]{0:T(128)S(1)} %reshape.336), kind=kCustom, calls=%fused_computation | custom fusion | bytes 960 | tf_op jit(solution)/shard_map/gather | solution.py:101
  14.6 0.1 reshape.339
  14.7 0.0 copy-done
  14.7 0.1 dynamic-slice_bitcast_fusion
  14.8 0.2 multiply_reduce_fusion
  14.9 0.2 select_reduce_fusion
  15.1 0.6 fusion.65
  17.5 0.2 fusion.24
  17.8 1.2 %constant_dynamic-slice_fusion.2 = (f32[256,256]{1,0:T(8,128)S(1)}, f32[256,256]{1,0:T(8,128)S(1)}, f32[256,256]{1,0:T(8,128)S(1)}) fusion(f32[3840,256]{1,0:T(8,128)} %param.5, s32[]{:T(128)S(6)} %select_n.168, s32[]{:T(128)S(6)} %select_n.170, s32[]{:T(128)S(6)} %select_n.169), kind=kLoop, calls=%fused_computation.71 | loop fusion | bytes 1572876 | tf_op jit(solution)/shard_map/dynamic_slice | solution.py:37
  18.9 0.1 pad_maximum_fusion
  19.0 0.0 collective-permute-done.2
  19.0 0.0 collective-permute-done
  19.0 0.0 collective-permute-done.1
  19.1 3.5 %collective-permute-start.3 = (f32[64,768]{1,0:T(8,128)S(1)}, f32[64,768]{1,0:T(8,128)S(1)}, u32[]{:S(2)}, u32[]{:S(2)}) collective-permute-start(f32[64,768]{1,0:T(8,128)S(1)} %add_select_fusion), channel_id=1, source_target_pairs={{0,0},{15,16},{14,32},{13,48},{64,64},{79,80},{78,96},{77,112},{12... | collective-permute-start | bytes 589832 | tf_op jit(solution)/shard_map/ppermute | solution.py:79
  22.6 4.6 %collective-permute-start.4 = (f32[64,768]{1,0:T(8,128)S(1)}, f32[64,768]{1,0:T(8,128)S(1)}, u32[]{:S(2)}, u32[]{:S(2)}) collective-permute-start(f32[64,768]{1,0:T(8,128)S(1)} %add_select_fusion), channel_id=1, source_target_pairs={{0,32},{15,48},{14,0},{13,16},{64,96},{79,112},{78,64},{77,80},{12... | collective-permute-start | bytes 589832 | tf_op jit(solution)/shard_map/ppermute | solution.py:79
  27.2 1.5 %fusion.2 = f32[3,256,256]{2,0,1:T(4,128)S(1)} fusion(f32[3,256,256]{2,1,0:T(8,128)S(1)} %bitcast.77, s32[3]{0:T(128)S(1)} %get-tuple-element.19, pred[3]{0:T(512)(128)(4,1)S(1)} %get-tuple-element.26, s32[3]{0:T(128)S(1)} %get-tuple-element.16, pred[3]{0:T(512)(128)(4,1)S(1)} %get-tuple-element.29), kind=kOutput, calls=%fused_computation.4 | convolution fusion | flops 7077915 | bytes 1572894 | tf_op jit(solution)/shard_map/ij,jab->iab/dot_general | solution.py:44
  28.7 17.2 %collective-permute-done.3 = f32[64,768]{1,0:T(8,128)S(1)} collective-permute-done((f32[64,768]{1,0:T(8,128)S(1)}, f32[64,768]{1,0:T(8,128)S(1)}, u32[]{:S(2)}, u32[]{:S(2)}) %collective-permute-start.3) | collective-permute-done | bytes 196640 | tf_op jit(solution)/shard_map/ppermute | solution.py:79
  45.9 0.0 collective-permute-done.4
  45.9 0.8 %pad_maximum_fusion.1 = f32[2,64,768]{2,1,0:T(8,128)} fusion(f32[1,64,768]{2,1,0:T(8,128)S(1)} %bitcast.85, f32[1,64,768]{2,1,0:T(8,128)S(1)} %bitcast.86), kind=kLoop, calls=%fused_computation.13 | loop fusion | flops 98304 | bytes 786432 | tf_op jit(solution)/shard_map/stack | solution.py:120
  46.7 0.0 collective-permute-start.5
  46.7 1.5 %fusion.4 = f32[3,256,256]{2,0,1:T(4,128)S(1)} fusion(f32[3,256,256]{2,1,0:T(8,128)S(1)} %bitcast.78, s32[3]{0:T(128)S(1)} %get-tuple-element.19, pred[3]{0:T(512)(128)(4,1)S(1)} %get-tuple-element.27, s32[3]{0:T(128)S(1)} %get-tuple-element.17, pred[3]{0:T(512)(128)(4,1)S(1)} %get-tuple-element.29), kind=kOutput, calls=%fused_computation.6 | convolution fusion | flops 7077915 | bytes 1572894 | tf_op jit(solution)/shard_map/ij,jab->iab/dot_general | solution.py:44
  48.2 1.0 %copy.20 = f32[3,256,256]{2,1,0:T(8,128)} copy(f32[3,256,256]{2,0,1:T(4,128)S(1)} %fusion.2) | data formatting | bytes 1572864 | tf_op jit(solution)/shard_map/ij,jab->iab/dot_general | solution.py:44
  49.3 0.0 copy-start.1
  49.3 0.2 copy.18
  49.4 1.5 %fusion.6 = f32[3,256,256]{2,0,1:T(4,128)S(1)} fusion(f32[3,256,256]{2,1,0:T(8,128)S(1)} %bitcast.79, s32[3]{0:T(128)S(1)} %get-tuple-element.19, pred[3]{0:T(512)(128)(4,1)S(1)} %get-tuple-element.28, s32[3]{0:T(128)S(1)} %get-tuple-element.18, pred[3]{0:T(512)(128)(4,1)S(1)} %get-tuple-element.29), kind=kOutput, calls=%fused_computation.8 | convolution fusion | flops 7077915 | bytes 1572894 | tf_op jit(solution)/shard_map/ij,jab->iab/dot_general | solution.py:44
  50.9 0.2 copy.16
  51.1 0.0 collective-permute-done.5
  51.1 0.0 copy-done.1
  51.1 1.4 %fusion.10 = f32[64,256]{1,0:T(8,128)S(1)} fusion(f32[768,256]{1,0:T(8,128)S(1)} %bitcast.81, f32[64,768]{1,0:T(8,128)S(1)} %get-tuple-element.14, f32[2,64,768]{2,1,0:T(8,128)} %collective-permute-done.5, pred[]{:T(512)S(6)} %eq.124), kind=kOutput, calls=%fused_computation.17 | convolution fusion | flops 151044096 | bytes 1245185 | tf_op jit(solution)/shard_map/dot_general | solution.py:131
  52.6 6.4 %collective-permute-start.8 = (f32[64,256]{1,0:T(8,128)S(1)}, f32[64,256]{1,0:T(8,128)S(1)}, u32[]{:S(2)}, u32[]{:S(2)}) collective-permute-start(f32[64,256]{1,0:T(8,128)S(1)} %fusion.10), channel_id=1, source_target_pairs={{0,13},{1,14},{2,15},{3,0},{4,1},{5,2},{6,3},{7,4},{8,5},{9,6},{10... | collective-permute-start | bytes 196616 | tf_op jit(solution)/shard_map/ppermute | solution.py:15
  59.0 1.4 %fusion.12 = f32[64,256]{1,0:T(8,128)S(1)} fusion(f32[768,256]{1,0:T(8,128)S(1)} %bitcast.83, f32[64,768]{1,0:T(8,128)S(1)} %get-tuple-element.14, f32[2,64,768]{2,1,0:T(8,128)} %collective-permute-done.5, pred[]{:T(512)S(6)} %eq.124), kind=kOutput, calls=%fused_computation.19 | convolution fusion | flops 151044096 | bytes 1245185 | tf_op jit(solution)/shard_map/dot_general | solution.py:131
  60.4 2.2 %collective-permute-start.7 = (f32[64,256]{1,0:T(8,128)S(1)}, f32[64,256]{1,0:T(8,128)S(1)}, u32[]{:S(2)}, u32[]{:S(2)}) collective-permute-start(f32[64,256]{1,0:T(8,128)S(1)} %fusion.12), channel_id=1, source_target_pairs={{0,14},{1,15},{2,0},{3,1},{4,2},{5,3},{6,4},{7,5},{8,6},{9,7},{10,... | collective-permute-start | bytes 196616 | tf_op jit(solution)/shard_map/ppermute | solution.py:15
  62.6 1.4 %fusion.14 = f32[64,256]{1,0:T(8,128)S(1)} fusion(f32[768,256]{1,0:T(8,128)S(1)} %bitcast.82, f32[64,768]{1,0:T(8,128)S(1)} %get-tuple-element.13, f32[2,64,768]{2,1,0:T(8,128)} %collective-permute-done.5, pred[]{:T(512)S(6)} %eq.124), kind=kOutput, calls=%fused_computation.21 | convolution fusion | flops 151044096 | bytes 1245185 | tf_op jit(solution)/shard_map/dot_general | solution.py:131
  64.0 0.1 collective-permute-start.6
  64.1 1.5 %fusion.8 = f32[3,256,256]{2,0,1:T(4,128)S(1)} fusion(f32[3,256,256]{2,1,0:T(8,128)S(1)} %bitcast.80, s32[3]{0:T(128)S(1)} %get-tuple-element.19, pred[3]{0:T(512)(128)(4,1)S(1)} %get-tuple-element.29, pred[3]{0:T(512)(128)(4,1)S(1)} %get-tuple-element.25, s32[3]{0:T(128)S(1)} %get-tuple-element.15), kind=kOutput, calls=%fused_computation.10 | convolution fusion | flops 7077915 | bytes 1572894 | tf_op jit(solution)/shard_map/ij,jab->iab/dot_general | solution.py:44
  65.6 0.2 copy.14
  65.8 0.0 collective-permute-done.8
  65.8 1.7 %collective-permute-done.7 = f32[64,256]{1,0:T(8,128)S(1)} collective-permute-done((f32[64,256]{1,0:T(8,128)S(1)}, f32[64,256]{1,0:T(8,128)S(1)}, u32[]{:S(2)}, u32[]{:S(2)}) %collective-permute-start.7) | collective-permute-done | bytes 65568 | tf_op jit(solution)/shard_map/ppermute | solution.py:15
  67.5 0.6 collective-permute-done.6
  68.1 2.1 %fusion.1 = f32[64,256]{1,0:T(8,128)} fusion(f32[64,256]{1,0:T(8,128)S(1)} %collective-permute-done.8, f32[64,256]{1,0:T(8,128)S(1)} %collective-permute-done.7, f32[64,256]{1,0:T(8,128)S(1)} %collective-permute-done.6, f32[768,256]{1,0:T(8,128)S(1)} %bitcast.84, f32[64,768]{1,0:T(8,128)S(1)} %get-tuple-element.13, ...), kind=kOutput, calls=%fused_computation.3 | convolution fusion | flops 151093248 | bytes 1441793 | tf_op jit(solution)/shard_map/dot_general | solution.py:131
  (8 shorter events, 0.1 us)
Async XLA Ops:
  0.0 14.7 %copy-start = (s32[240,16]{0,1:T(8,128)S(1)}, s32[240,16]{0,1:T(8,128)}, u32[]{:S(2)}) copy-start(s32[240,16]{0,1:T(8,128)} %param.7) | copy-start | bytes 46084
  4.7 14.3 %collective-permute-start.2 = (f32[64,768]{1,0:T(8,128)S(1)}, f32[64,768]{1,0:T(8,128)S(1)}, u32[]{:S(2)}, u32[]{:S(2)}) collective-permute-start(f32[64,768]{1,0:T(8,128)S(1)} %pad_maximum_fusion.2), channel_id=1, source_target_pairs={{0,192},{16,208},{32,224},{48,240},{17,209},{33,225},{49,241},{65,... | collective-permute-start | bytes 589832 | tf_op jit(solution)/shard_map/ppermute | solution.py:61
  9.9 9.1 %collective-permute-start = (f32[64,768]{1,0:T(8,128)S(1)}, f32[64,768]{1,0:T(8,128)S(1)}, u32[]{:S(2)}, u32[]{:S(2)}) collective-permute-start(f32[64,768]{1,0:T(8,128)S(1)} %pad_maximum_fusion.2), channel_id=1, source_target_pairs={{0,64},{16,80},{32,96},{48,112},{17,81},{33,97},{49,113},{65,129},... | collective-permute-start | bytes 589832 | tf_op jit(solution)/shard_map/ppermute | solution.py:61
  11.2 7.8 %collective-permute-start.1 = (f32[64,768]{1,0:T(8,128)S(1)}, f32[64,768]{1,0:T(8,128)S(1)}, u32[]{:S(2)}, u32[]{:S(2)}) collective-permute-start(f32[64,768]{1,0:T(8,128)S(1)} %pad_maximum_fusion.2), channel_id=1, source_target_pairs={{0,128},{16,144},{32,160},{48,176},{17,145},{33,161},{49,177},{65,... | collective-permute-start | bytes 589832 | tf_op jit(solution)/shard_map/ppermute | solution.py:61
  19.1 26.8 %collective-permute-start.3 = (f32[64,768]{1,0:T(8,128)S(1)}, f32[64,768]{1,0:T(8,128)S(1)}, u32[]{:S(2)}, u32[]{:S(2)}) collective-permute-start(f32[64,768]{1,0:T(8,128)S(1)} %add_select_fusion), channel_id=1, source_target_pairs={{0,0},{15,16},{14,32},{13,48},{64,64},{79,80},{78,96},{77,112},{12... | collective-permute-start | bytes 589832 | tf_op jit(solution)/shard_map/ppermute | solution.py:79
  22.6 23.3 %collective-permute-start.4 = (f32[64,768]{1,0:T(8,128)S(1)}, f32[64,768]{1,0:T(8,128)S(1)}, u32[]{:S(2)}, u32[]{:S(2)}) collective-permute-start(f32[64,768]{1,0:T(8,128)S(1)} %add_select_fusion), channel_id=1, source_target_pairs={{0,32},{15,48},{14,0},{13,16},{64,96},{79,112},{78,64},{77,80},{12... | collective-permute-start | bytes 589832 | tf_op jit(solution)/shard_map/ppermute | solution.py:79
  46.7 4.4 %collective-permute-start.5 = (f32[2,64,768]{2,1,0:T(8,128)}, f32[2,64,768]{2,1,0:T(8,128)}, u32[]{:S(2)}, u32[]{:S(2)}) collective-permute-start(f32[2,64,768]{2,1,0:T(8,128)} %pad_maximum_fusion.1), channel_id=1, source_target_pairs={{0,16},{16,0},{32,48},{48,32},{64,80},{80,64},{96,112},{112,96},{1... | collective-permute-start | bytes 1179656 | tf_op jit(solution)/shard_map/ppermute | solution.py:120
  49.3 1.8 %copy-start.1 = (f32[3,256,256]{2,1,0:T(8,128)S(1)}, f32[3,256,256]{2,1,0:T(8,128)}, u32[]{:S(2)}) copy-start(f32[3,256,256]{2,1,0:T(8,128)} %copy.20) | copy-start | bytes 2359300
  52.6 13.2 %collective-permute-start.8 = (f32[64,256]{1,0:T(8,128)S(1)}, f32[64,256]{1,0:T(8,128)S(1)}, u32[]{:S(2)}, u32[]{:S(2)}) collective-permute-start(f32[64,256]{1,0:T(8,128)S(1)} %fusion.10), channel_id=1, source_target_pairs={{0,13},{1,14},{2,15},{3,0},{4,1},{5,2},{6,3},{7,4},{8,5},{9,6},{10... | collective-permute-start | bytes 196616 | tf_op jit(solution)/shard_map/ppermute | solution.py:15
  60.4 7.1 %collective-permute-start.7 = (f32[64,256]{1,0:T(8,128)S(1)}, f32[64,256]{1,0:T(8,128)S(1)}, u32[]{:S(2)}, u32[]{:S(2)}) collective-permute-start(f32[64,256]{1,0:T(8,128)S(1)} %fusion.12), channel_id=1, source_target_pairs={{0,14},{1,15},{2,0},{3,1},{4,2},{5,3},{6,4},{7,5},{8,6},{9,7},{10,... | collective-permute-start | bytes 196616 | tf_op jit(solution)/shard_map/ppermute | solution.py:15
  64.0 4.1 %collective-permute-start.6 = (f32[64,256]{1,0:T(8,128)S(1)}, f32[64,256]{1,0:T(8,128)S(1)}, u32[]{:S(2)}, u32[]{:S(2)}) collective-permute-start(f32[64,256]{1,0:T(8,128)S(1)} %fusion.14), channel_id=1, source_target_pairs={{0,15},{1,0},{2,1},{3,2},{4,3},{5,4},{6,5},{7,6},{8,7},{9,8},{10,9... | collective-permute-start | bytes 196616 | tf_op jit(solution)/shard_map/ppermute | solution.py:15

commit v4 on v1

--- a/solution.py
+++ b/solution.py
@@ -98,19 +98,17 @@
     core = rowdev % 2
     yhi = (rowdev // 2) % 2
 
-    grid_rows = jnp.stack([coldev] + [(coldev - k) % ncol for k in range(STEPS)])
-    panels = jnp.stack([rowdev] + [coldev] * STEPS)
-    lefts = left_pattern[grid_rows[:, None], panels[:, None] * per_k + jnp.arange(per_k)[None, :]]
+    own_flags = lax.dynamic_slice(left_pattern, (coldev, rowdev * per_k), (1, per_k))
+    own_left = slots(own_flags, CAP)[0][0]
+    grid_rows = jnp.stack([(coldev - k) % ncol for k in range(STEPS)])
+    lefts = left_pattern[grid_rows[:, None], coldev * per_k + jnp.arange(per_k)[None, :]]
     own_right = lax.dynamic_slice(right_pattern, (coldev * trows, rowdev), (trows, 1)).reshape(1, trows)
-    flags = jnp.concatenate([lefts, own_right], axis=0)
-    index, ok = slots(flags, CAP)
-    own_left = index[0]
-    lidx, lok = index[1:1 + STEPS], ok[1:1 + STEPS]
-    ridx, rok = index[1 + STEPS], ok[1 + STEPS]
+    index, ok = slots(jnp.concatenate([lefts, own_right], axis=0), CAP)
+    lidx, lok = index[:STEPS], ok[:STEPS]
+    ridx, rok = index[STEPS], ok[STEPS]
 
     left_small = pick_cols(left_rows, own_left, blk)
     right_small = pick_rows(right_cols, ridx, blk)
-    highest = lax.Precision.HIGHEST
 
     def ordered_for(k):
         kl = lax.dynamic_index_in_dim(lidx, k, axis=0, keepdims=False)
@@ -128,7 +126,7 @@
     total = None
     for near_k, to_partner, right in plans:
         left = near if near_k == 0 else far
-        part = jnp.dot(left, right, precision=highest, preferred_element_type=jnp.float32)
+        part = jnp.dot(left, right, precision=lax.Precision.HIGH, preferred_element_type=jnp.float32)
         part = send_home(part, near_k, to_partner, nrow, ncol)
         total = part if total is None else total + part
     return total

time: 80.2 us -> 78.9 us (0.984)
  the two profiles are of different devices: /device:TPU:9 before, /device:TPU:24 now
where the time goes in v4:
time: 78.9 us; the launch traced here: 78.5 us
  starting transfers between devices  30.8 us (39%)
  waiting for transfers between devices  25.4 us (32%)
  matrix products  7.42 us (9%)
  local copies, waits for them, and re-layouts  5.68 us (7%)
  other arithmetic  5.15 us (7%)
  between operations  4.05 us (5%)
    ppermute x4, starting transfers between devices, send_home(): return lax.ppermute(part, flat, flat_pairs(moves, ncol))  18 us
    ppermute x3, waiting for transfers between devices, spread_roots(): received.append(lax.ppermute(left_small, flat, flat_pairs(moves, ncol)))  10.2 us
    ppermute x2, starting transfers between devices, gather_lefts(): received.append(lax.ppermute(held, flat, flat_pairs(moves, ncol)))  8.77 us
    ppermute x2, waiting for transfers between devices, gather_lefts(): received.append(lax.ppermute(held, flat, flat_pairs(moves, ncol)))  7.69 us
    ppermute x4, waiting for transfers between devices, send_home(): return lax.ppermute(part, flat, flat_pairs(moves, ncol))  7.49 us
    dot_general x4, matrix products, aligned_right(): jnp.einsum('ij,jab->iab', weight, blocks, precision=lax.Precision.HIGHEST)  5.99 us
    ppermute x3, starting transfers between devices, spread_roots(): received.append(lax.ppermute(left_small, flat, flat_pairs(moves, ncol)))  3.98 us
  transfers between devices with their start and end apart: 10, of which 4 were waited for; matrix products, arithmetic and copies ran while one was open for 11% of the time, Pallas kernels for 0%

profile of v4, /device:TPU:24, one launch (start us, length us, event | category | flops | bytes accessed | tf_op | source)
XLA Modules:
  0.0 78.5 jit_solution(9943338102174694059)
XLA Ops:
  0.0 0.0 copy-start
  0.0 0.0 copy-start.1
  0.1 0.1 fusion.56
  0.2 0.1 broadcast_or_fusion
  0.2 0.1 reshape.328
  0.3 0.4 copy-done.1
  0.7 1.0 %gather_fusion = s32[60]{0:T(128)S(1)} fusion(s32[16,240]{1,0:T(8,128)S(1)} %copy-done.1, s32[60]{0:T(128)S(1)} %reshape.328), kind=kCustom, calls=%fused_computation | custom fusion | bytes 960 | tf_op jit(solution)/shard_map/gather | solution.py:104
  1.8 0.1 reshape.331
  1.9 0.0 copy-done
  1.9 0.1 dynamic-slice_bitcast_fusion
  2.0 0.2 multiply_reduce_fusion
  2.1 0.2 select_reduce_fusion
  2.3 0.6 fusion.64
  4.7 0.2 fusion.15
  5.0 1.2 %constant_dynamic-slice_fusion.8 = (f32[256,256]{1,0:T(8,128)S(1)}, f32[256,256]{1,0:T(8,128)S(1)}, f32[256,256]{1,0:T(8,128)S(1)}) fusion(f32[3840,256]{1,0:T(8,128)} %param.5, s32[]{:T(128)S(6)} %select_n.156, s32[]{:T(128)S(6)} %select_n.158, s32[]{:T(128)S(6)} %select_n.157), kind=kLoop, calls=%fused_computation.42 | loop fusion | bytes 1572876 | tf_op jit(solution)/shard_map/dynamic_slice | solution.py:31
  6.2 0.1 pad_maximum_fusion.1
  6.2 1.5 %fusion.2 = f32[3,256,256]{2,0,1:T(4,128)S(1)} fusion(f32[3,256,256]{2,1,0:T(8,128)S(1)} %bitcast.63, s32[3]{0:T(128)S(1)} %get-tuple-element.30, pred[3]{0:T(512)(128)(4,1)S(1)} %get-tuple-element.24, s32[3]{0:T(128)S(1)} %get-tuple-element.20, pred[3]{0:T(512)(128)(4,1)S(1)} %get-tuple-element.29), kind=kOutput, calls=%fused_computation.4 | convolution fusion | flops 7077915 | bytes 1572894 | tf_op jit(solution)/shard_map/ij,jab->iab/dot_general | solution.py:38
  7.7 0.2 copy.18
  7.9 1.5 %fusion = f32[3,256,256]{2,0,1:T(4,128)S(1)} fusion(f32[3,256,256]{2,1,0:T(8,128)S(1)} %bitcast.64, s32[3]{0:T(128)S(1)} %get-tuple-element.30, pred[3]{0:T(512)(128)(4,1)S(1)} %get-tuple-element.23, s32[3]{0:T(128)S(1)} %get-tuple-element.19, pred[3]{0:T(512)(128)(4,1)S(1)} %get-tuple-element.29), kind=kOutput, calls=%fused_computation.2 | convolution fusion | flops 7077915 | bytes 1572894 | tf_op jit(solution)/shard_map/ij,jab->iab/dot_general | solution.py:38
  9.4 0.2 copy.20
  9.5 1.3 %pad_maximum_fusion = f32[2,768,256]{2,1,0:T(8,128)} fusion(f32[1,768,256]{2,1,0:T(8,128)S(1)} %bitcast.70, f32[1,768,256]{2,1,0:T(8,128)S(1)} %bitcast.69), kind=kLoop, calls=%fused_computation.1 | loop fusion | flops 393216 | bytes 3145728 | tf_op jit(solution)/shard_map/stack | solution.py:118
  10.8 0.0 collective-permute-start.7
  10.8 0.1 broadcast_compare_fusion.1
  10.9 0.4 fusion.14
  11.3 0.2 fusion.37
  11.4 0.6 fusion.65
  14.0 0.9 %constant_dynamic-slice_fusion.13 = (f32[64,256]{1,0:T(8,128)S(1)}, f32[64,256]{1,0:T(8,128)S(1)}, f32[64,256]{1,0:T(8,128)S(1)}) fusion(f32[64,3840]{1,0:T(8,128)} %param.4, s32[]{:T(128)S(6)} %select_n.140, s32[]{:T(128)S(6)} %select_n.142, s32[]{:T(128)S(6)} %select_n.141), kind=kLoop, calls=%fused_computation.47 | loop fusion | bytes 393228 | tf_op jit(solution)/shard_map/dynamic_slice | solution.py:25
  14.9 0.7 pad_maximum_fusion.2
  15.6 1.3 %collective-permute-start = (f32[64,768]{1,0:T(8,128)}, f32[64,768]{1,0:T(8,128)}, u32[]{:S(2)}, u32[]{:S(2)}) collective-permute-start(f32[64,768]{1,0:T(8,128)} %pad_maximum_fusion.2), channel_id=1, source_target_pairs={{0,64},{16,80},{32,96},{48,112},{17,81},{33,97},{49,113},{65,129},... | collective-permute-start | bytes 589832 | tf_op jit(solution)/shard_map/ppermute | solution.py:55
  16.9 1.3 %collective-permute-start.1 = (f32[64,768]{1,0:T(8,128)}, f32[64,768]{1,0:T(8,128)}, u32[]{:S(2)}, u32[]{:S(2)}) collective-permute-start(f32[64,768]{1,0:T(8,128)} %pad_maximum_fusion.2), channel_id=1, source_target_pairs={{0,128},{16,144},{32,160},{48,176},{17,145},{33,161},{49,177},{65,... | collective-permute-start | bytes 589832 | tf_op jit(solution)/shard_map/ppermute | solution.py:55
  18.2 1.4 %collective-permute-start.2 = (f32[64,768]{1,0:T(8,128)}, f32[64,768]{1,0:T(8,128)}, u32[]{:S(2)}, u32[]{:S(2)}) collective-permute-start(f32[64,768]{1,0:T(8,128)} %pad_maximum_fusion.2), channel_id=1, source_target_pairs={{0,192},{16,208},{32,224},{48,240},{17,209},{33,225},{49,241},{65,... | collective-permute-start | bytes 589832 | tf_op jit(solution)/shard_map/ppermute | solution.py:55
  19.6 1.5 %fusion.4 = f32[3,256,256]{2,0,1:T(4,128)S(1)} fusion(f32[3,256,256]{2,1,0:T(8,128)S(1)} %bitcast.65, s32[3]{0:T(128)S(1)} %get-tuple-element.30, pred[3]{0:T(512)(128)(4,1)S(1)} %get-tuple-element.22, s32[3]{0:T(128)S(1)} %get-tuple-element.18, pred[3]{0:T(512)(128)(4,1)S(1)} %get-tuple-element.29), kind=kOutput, calls=%fused_computation.6 | convolution fusion | flops 7077915 | bytes 1572894 | tf_op jit(solution)/shard_map/ij,jab->iab/dot_general | solution.py:38
  21.1 0.2 copy.16
  21.3 0.0 collective-permute-done
  21.3 10.2 %collective-permute-done.1 = f32[64,768]{1,0:T(8,128)} collective-permute-done((f32[64,768]{1,0:T(8,128)}, f32[64,768]{1,0:T(8,128)}, u32[]{:S(2)}, u32[]{:S(2)}) %collective-permute-start.1) | collective-permute-done | bytes 196640 | tf_op jit(solution)/shard_map/ppermute | solution.py:55
  31.5 0.0 collective-permute-done.2
  31.5 1.2 %add_select_fusion = f32[64,768]{1,0:T(8,128)S(1)} fusion(f32[64,768]{1,0:T(8,128)} %collective-permute-done.2, f32[64,768]{1,0:T(8,128)} %collective-permute-done, f32[64,768]{1,0:T(8,128)} %collective-permute-done.1, pred[]{:T(512)S(6)} %lt.132, f32[64,256]{1,0:T(8,128)S(1)} %get-tuple-element.11, f32[64,256]{1,0:T(8,128)S(1)} %get-tuple-element.12, ...), kind=kLoop, calls=%fused_computation.16 | loop fusion | flops 245760 | bytes 983041 | tf_op jit(solution)/shard_map/jit(_where)/select_n | solution.py:60
  32.7 5.2 %collective-permute-start.3 = (f32[64,768]{1,0:T(8,128)S(1)}, f32[64,768]{1,0:T(8,128)S(1)}, u32[]{:S(2)}, u32[]{:S(2)}) collective-permute-start(f32[64,768]{1,0:T(8,128)S(1)} %add_select_fusion), channel_id=1, source_target_pairs={{0,0},{15,16},{14,32},{13,48},{64,64},{79,80},{78,96},{77,112},{12... | collective-permute-start | bytes 589832 | tf_op jit(solution)/shard_map/ppermute | solution.py:73
  37.9 3.6 %collective-permute-start.4 = (f32[64,768]{1,0:T(8,128)S(1)}, f32[64,768]{1,0:T(8,128)S(1)}, u32[]{:S(2)}, u32[]{:S(2)}) collective-permute-start(f32[64,768]{1,0:T(8,128)S(1)} %add_select_fusion), channel_id=1, source_target_pairs={{0,32},{15,48},{14,0},{13,16},{64,96},{79,112},{78,64},{77,80},{12... | collective-permute-start | bytes 589832 | tf_op jit(solution)/shard_map/ppermute | solution.py:73
  41.5 1.5 %fusion.6 = f32[3,256,256]{2,0,1:T(4,128)S(1)} fusion(f32[3,256,256]{2,1,0:T(8,128)S(1)} %bitcast.66, s32[3]{0:T(128)S(1)} %get-tuple-element.30, pred[3]{0:T(512)(128)(4,1)S(1)} %get-tuple-element.29, pred[3]{0:T(512)(128)(4,1)S(1)} %get-tuple-element.25, s32[3]{0:T(128)S(1)} %get-tuple-element.21), kind=kOutput, calls=%fused_computation.8 | convolution fusion | flops 7077915 | bytes 1572894 | tf_op jit(solution)/shard_map/ij,jab->iab/dot_general | solution.py:38
  43.0 0.2 copy.14
  43.2 7.7 %collective-permute-done.3 = f32[64,768]{1,0:T(8,128)S(1)} collective-permute-done((f32[64,768]{1,0:T(8,128)S(1)}, f32[64,768]{1,0:T(8,128)S(1)}, u32[]{:S(2)}, u32[]{:S(2)}) %collective-permute-start.3) | collective-permute-done | bytes 196640 | tf_op jit(solution)/shard_map/ppermute | solution.py:73
  50.9 0.0 collective-permute-done.4
  50.9 0.4 fusion.11
  51.2 2.8 %collective-permute-start.6 = (f32[64,256]{1,0:T(8,128)S(1)}, f32[64,256]{1,0:T(8,128)S(1)}, u32[]{:S(2)}, u32[]{:S(2)}) collective-permute-start(f32[64,256]{1,0:T(8,128)S(1)} %fusion.11), channel_id=1, source_target_pairs={{0,14},{1,15},{2,0},{3,1},{4,2},{5,3},{6,4},{7,5},{8,6},{9,7},{10,... | collective-permute-start | bytes 196616 | tf_op jit(solution)/shard_map/ppermute | solution.py:85
  54.0 0.4 fusion.10
  54.3 0.7 collective-permute-start.5
  55.0 0.0 collective-permute-done.7
  55.0 0.4 fusion.9
  55.4 14.5 %collective-permute-start.8 = (f32[64,256]{1,0:T(8,128)S(1)}, f32[64,256]{1,0:T(8,128)S(1)}, u32[]{:S(2)}, u32[]{:S(2)}) collective-permute-start(f32[64,256]{1,0:T(8,128)S(1)} %fusion.9), channel_id=1, source_target_pairs={{0,16},{1,17},{2,18},{3,19},{4,20},{5,21},{6,22},{7,23},{8,24},{9,... | collective-permute-start | bytes 196616 | tf_op jit(solution)/shard_map/ppermute | solution.py:85
  69.9 0.4 fusion.8
  70.3 0.1 collective-permute-start.9
  70.4 0.0 collective-permute-done.6
  70.4 0.0 collective-permute-done.5
  70.4 0.4 collective-permute-done.8
  70.8 7.1 %collective-permute-done.9 = f32[64,256]{1,0:T(8,128)S(1)} collective-permute-done((f32[64,256]{1,0:T(8,128)S(1)}, f32[64,256]{1,0:T(8,128)S(1)}, u32[]{:S(2)}, u32[]{:S(2)}) %collective-permute-start.9) | collective-permute-done | bytes 65568 | tf_op jit(solution)/shard_map/ppermute | solution.py:85
  77.9 0.6 add_add_fusion
  (7 shorter events, 0.1 us)
Async XLA Ops:
  0.0 1.9 %copy-start = (s32[240,16]{0,1:T(8,128)S(1)}, s32[240,16]{0,1:T(8,128)}, u32[]{:S(2)}) copy-start(s32[240,16]{0,1:T(8,128)} %param.7) | copy-start | bytes 46084
  0.0 0.7 copy-start.1
  10.8 44.2 %collective-permute-start.7 = (f32[2,768,256]{2,1,0:T(8,128)}, f32[2,768,256]{2,1,0:T(8,128)S(1)}, u32[]{:S(2)}, u32[]{:S(2)}) collective-permute-start(f32[2,768,256]{2,1,0:T(8,128)} %pad_maximum_fusion), channel_id=1, source_target_pairs={{0,16},{16,0},{32,48},{48,32},{64,80},{80,64},{96,112},{112,96},{1... | collective-permute-start | bytes 4718600 | tf_op jit(solution)/shard_map/ppermute | solution.py:119
  15.6 5.7 %collective-permute-start = (f32[64,768]{1,0:T(8,128)}, f32[64,768]{1,0:T(8,128)}, u32[]{:S(2)}, u32[]{:S(2)}) collective-permute-start(f32[64,768]{1,0:T(8,128)} %pad_maximum_fusion.2), channel_id=1, source_target_pairs={{0,64},{16,80},{32,96},{48,112},{17,81},{33,97},{49,113},{65,129},... | collective-permute-start | bytes 589832 | tf_op jit(solution)/shard_map/ppermute | solution.py:55
  16.9 14.6 %collective-permute-start.1 = (f32[64,768]{1,0:T(8,128)}, f32[64,768]{1,0:T(8,128)}, u32[]{:S(2)}, u32[]{:S(2)}) collective-permute-start(f32[64,768]{1,0:T(8,128)} %pad_maximum_fusion.2), channel_id=1, source_target_pairs={{0,128},{16,144},{32,160},{48,176},{17,145},{33,161},{49,177},{65,... | collective-permute-start | bytes 589832 | tf_op jit(solution)/shard_map/ppermute | solution.py:55
  18.2 13.3 %collective-permute-start.2 = (f32[64,768]{1,0:T(8,128)}, f32[64,768]{1,0:T(8,128)}, u32[]{:S(2)}, u32[]{:S(2)}) collective-permute-start(f32[64,768]{1,0:T(8,128)} %pad_maximum_fusion.2), channel_id=1, source_target_pairs={{0,192},{16,208},{32,224},{48,240},{17,209},{33,225},{49,241},{65,... | collective-permute-start | bytes 589832 | tf_op jit(solution)/shard_map/ppermute | solution.py:55
  32.7 18.2 %collective-permute-start.3 = (f32[64,768]{1,0:T(8,128)S(1)}, f32[64,768]{1,0:T(8,128)S(1)}, u32[]{:S(2)}, u32[]{:S(2)}) collective-permute-start(f32[64,768]{1,0:T(8,128)S(1)} %add_select_fusion), channel_id=1, source_target_pairs={{0,0},{15,16},{14,32},{13,48},{64,64},{79,80},{78,96},{77,112},{12... | collective-permute-start | bytes 589832 | tf_op jit(solution)/shard_map/ppermute | solution.py:73
  37.9 13.0 %collective-permute-start.4 = (f32[64,768]{1,0:T(8,128)S(1)}, f32[64,768]{1,0:T(8,128)S(1)}, u32[]{:S(2)}, u32[]{:S(2)}) collective-permute-start(f32[64,768]{1,0:T(8,128)S(1)} %add_select_fusion), channel_id=1, source_target_pairs={{0,32},{15,48},{14,0},{13,16},{64,96},{79,112},{78,64},{77,80},{12... | collective-permute-start | bytes 589832 | tf_op jit(solution)/shard_map/ppermute | solution.py:73
  51.2 19.2 %collective-permute-start.6 = (f32[64,256]{1,0:T(8,128)S(1)}, f32[64,256]{1,0:T(8,128)S(1)}, u32[]{:S(2)}, u32[]{:S(2)}) collective-permute-start(f32[64,256]{1,0:T(8,128)S(1)} %fusion.11), channel_id=1, source_target_pairs={{0,14},{1,15},{2,0},{3,1},{4,2},{5,3},{6,4},{7,5},{8,6},{9,7},{10,... | collective-permute-start | bytes 196616 | tf_op jit(solution)/shard_map/ppermute | solution.py:85
  54.3 16.1 %collective-permute-start.5 = (f32[64,256]{1,0:T(8,128)S(1)}, f32[64,256]{1,0:T(8,128)S(1)}, u32[]{:S(2)}, u32[]{:S(2)}) collective-permute-start(f32[64,256]{1,0:T(8,128)S(1)} %fusion.10), channel_id=1, source_target_pairs={{0,0},{1,1},{2,2},{3,3},{4,4},{5,5},{6,6},{7,7},{8,8},{9,9},{10,10... | collective-permute-start | bytes 196616 | tf_op jit(solution)/shard_map/ppermute | solution.py:85
  55.4 15.4 %collective-permute-start.8 = (f32[64,256]{1,0:T(8,128)S(1)}, f32[64,256]{1,0:T(8,128)S(1)}, u32[]{:S(2)}, u32[]{:S(2)}) collective-permute-start(f32[64,256]{1,0:T(8,128)S(1)} %fusion.9), channel_id=1, source_target_pairs={{0,16},{1,17},{2,18},{3,19},{4,20},{5,21},{6,22},{7,23},{8,24},{9,... | collective-permute-start | bytes 196616 | tf_op jit(solution)/shard_map/ppermute | solution.py:85
  70.3 7.6 %collective-permute-start.9 = (f32[64,256]{1,0:T(8,128)S(1)}, f32[64,256]{1,0:T(8,128)S(1)}, u32[]{:S(2)}, u32[]{:S(2)}) collective-permute-start(f32[64,256]{1,0:T(8,128)S(1)} %fusion.8), channel_id=1, source_target_pairs={{0,30},{1,31},{2,16},{3,17},{4,18},{5,19},{6,20},{7,21},{8,22},{9,... | collective-permute-start | bytes 196616 | tf_op jit(solution)/shard_map/ppermute | solution.py:85
